TPU v7x, 512 devices: a whole 4x4x16 slice. The times are simulated.
512 devices in a mesh: group: 8 (over x, core), dev: 64 (over y, z).
Axes of the slice: x: 4, y: 4, z: 16, core: 2. Of those that a mesh axis runs over, the one named last changes fastest.
Arguments:
- probes: bfloat16 [2048, 32, 1024], P(('group', 'dev')), may hold values from -6 to 6
- points: float32 [2048, 3, 1024], P(('group', 'dev')), may hold values from -2.5 to 5.5
- leaf_order: int32 [2048, 1024], P(('group', 'dev')), may hold values from 0 to 1023, each once within a row
- leaf_basis: bfloat16 [2048, 1024, 256], P(('group', 'dev')), may hold values from -0.1875 to 0.1875
- node_transfer: bfloat16 [512, 4, 256, 256], P(('group', 'dev')), may hold values from -0.375 to 0.375
- group_transfer: bfloat16 [512, 256, 256], P(('group', 'dev')), may hold values from -0.375 to 0.375
- node_skeleton: float32 [512, 3, 256], P('group'), may hold values from 0 to 2
- group_skeleton: float32 [8, 3, 256], replicated, may hold values from 0 to 8
- near_pattern: int32 [2048, 5], P(('group', 'dev')), may hold values from 0 to 1, as said below
- node_coupling: int32 [512, 9], P(('group', 'dev')), may hold values 0 or 1
- signal_variance: float32 [], replicated, may hold values from 0.1 to 0.25
- noise_variance: float32 [], replicated, may hold values from 0.5 to 1.5
Outputs:
- applied: bfloat16 [2048, 32, 1024], P(('group', 'dev'))
Inputs may be any that keep to these rules, and one draw needn't show every extreme that they name: `leaf_order`: each row is a permutation. `near_pattern`: 1 marks a near-field block with the leaf at that offset; entries for leaves outside the set are not used. `node_coupling`: 1 marks a coupling with the node at that offset; entries with offsets under 2 or nodes outside the subtree are not used.
All inputs are finite; a program needn't handle non-finite values. No bound on the sum of `node_coupling` on one device may be relied on, other than what follows from the above.
Results may differ from a plain program's by a relative error of at most 0.012.
Values may be sent and summed in bfloat16 or wider, within the bound.
No kernel may reach another device: no remote copies, remote signals or barrier semaphores. Data moves between devices by JAX's collectives and lax.ppermute only.
A program may use at most 64 MiB of HBM per device.

v0:
```python
import functools

import jax
import jax.numpy as jnp
from jax import lax
from jax.sharding import Mesh
from jax.sharding import PartitionSpec as P

NEAR_REACH = 2
COUPLE_REACH = 4
GROUP_DEV = ("group", "dev_0", "dev_1")
DEV = ("dev_0", "dev_1")


ROOT_THREE = 1.7320508075688772
LENGTH_SCALE = 0.5


def with_halo(value, sides, width):
    edges = {}
    for axis, dim in sides:
        peers, length = (lax.axis_size(axis), value.shape[dim])
        up = [(i, (i + 1) % peers) for i in range(peers - 1)]
        last = lax.slice_in_dim(value, length - width, length, axis=dim)
        leading = lax.slice_in_dim(value, 0, width, axis=dim)
        edges[dim] = (
            lax.ppermute(last, axis, up),
            lax.ppermute(leading, axis, [(b, a) for a, b in up]),
        )
    done = []
    for _, dim in sides:
        low, high = edges[dim]
        around = [(width, width) if d in done else (0, 0) for d in range(value.ndim)]
        value = jnp.concatenate([jnp.pad(low, around), value, jnp.pad(high, around)], axis=dim)
        done.append(dim)
    return value


def by_axis(value, axes):
    return functools.reduce(lax.psum, axes, value)


def joined_along(pieces, dim):
    pieces = jnp.moveaxis(pieces, 0, dim)
    lengths = pieces.shape
    return pieces.reshape(*lengths[:dim], lengths[dim] * lengths[dim + 1], *lengths[dim + 2 :])


def from_everyone(value, axis):
    peers = lax.axis_size(axis)
    return lax.all_to_all(
        jnp.broadcast_to(value[None], (peers, *value.shape)), axis, 0, 0, tiled=True
    )


def collect(value, axis, dim):
    return joined_along(from_everyone(value, axis), dim)


def from_behind(block, axis, distance):
    devices = range(lax.axis_size(axis))
    route = [(i - distance, i) for i in devices if i - distance in devices]
    return lax.ppermute(block, axis, route)


def matern(source, target, amplitude):
    square = (source[0][:, None] - target[0][None, :]) ** 2
    square = square + (source[1][:, None] - target[1][None, :]) ** 2
    square = square + (source[2][:, None] - target[2][None, :]) ** 2
    scaled = jnp.sqrt(square) * (ROOT_THREE / LENGTH_SCALE)
    return (amplitude * (1.0 + scaled) * jnp.exp(-scaled)).astype(jnp.bfloat16)


def restore_leaf(values, ordering):
    return jnp.zeros_like(values).at[:, ordering].set(values)


def on_device(
    probes,
    points,
    leaf_order,
    leaf_basis,
    node_transfer,
    group_transfer,
    node_skeleton,
    group_skeleton,
    near_pattern,
    node_coupling,
    signal_variance,
    noise_variance,
):
    leaf_count, probe_count, leaf_size = probes.shape
    skeleton = leaf_basis.shape[2]
    window = 2 * NEAR_REACH + 1
    ordered = jnp.take_along_axis(probes, leaf_order[:, None, :], axis=2)
    wide_probes = with_halo(ordered, ((GROUP_DEV, 0),), NEAR_REACH)
    wide_points = with_halo(points, ((GROUP_DEV, 0),), NEAR_REACH)

    def near_leaf(item):
        position, pattern_row = item
        target = lax.dynamic_index_in_dim(wide_points, position + NEAR_REACH, 0, keepdims=False)
        summed = jnp.zeros((probe_count, leaf_size), jnp.float32)
        for offset in range(window):
            source = lax.dynamic_index_in_dim(wide_points, position + offset, 0, keepdims=False)
            values = lax.dynamic_index_in_dim(wide_probes, position + offset, 0, keepdims=False)
            kernel_tile = matern(source, target, signal_variance)
            contribution = jnp.dot(
                values, kernel_tile, preferred_element_type=jnp.float32
            ) * pattern_row[offset].astype(jnp.float32)
            summed = summed + contribution
        return summed

    near = lax.map(near_leaf, (jnp.arange(leaf_count, dtype=jnp.int32), near_pattern))
    leaf_coef = lax.dot_general(
        ordered, leaf_basis, (((2,), (1,)), ((0,), (0,))), preferred_element_type=jnp.float32
    ).astype(jnp.bfloat16)
    stacked = leaf_coef.transpose(1, 0, 2).reshape(probe_count, leaf_count * skeleton)
    transfer_flat = node_transfer[0].reshape(leaf_count * skeleton, skeleton)
    node_coef = jnp.dot(stacked, transfer_flat, preferred_element_type=jnp.float32).astype(
        jnp.bfloat16
    )
    group_term = jnp.dot(node_coef, group_transfer[0], preferred_element_type=jnp.float32)
    group_index = lax.axis_index("group")
    group_total = lax.axis_size("group")
    own_coef = by_axis(group_term, DEV).astype(jnp.bfloat16)
    group_coef = collect(own_coef[None], "group", 0)
    own_skeleton = lax.dynamic_index_in_dim(group_skeleton, group_index, 0, keepdims=False)
    far_group = jnp.zeros((probe_count, skeleton), jnp.float32)
    for other in range(group_total):
        kernel_tile = matern(group_skeleton[other], own_skeleton, signal_variance)
        contribution = jnp.dot(group_coef[other], kernel_tile, preferred_element_type=jnp.float32)
        far_group = far_group + jnp.where(other != group_index, contribution, jnp.float32(0.0))
    group_local = far_group.astype(jnp.bfloat16)
    node_index = lax.axis_index(DEV)
    node_total = lax.axis_size(DEV)
    own_node = lax.dynamic_index_in_dim(node_skeleton, node_index, 0, keepdims=False)
    relayed = {}
    lower_coef = node_coef
    upper_coef = node_coef
    for distance in range(1, COUPLE_REACH + 1):
        lower_coef = from_behind(lower_coef, DEV, 1)
        upper_coef = from_behind(upper_coef, DEV, -1)
        relayed[-distance] = lower_coef
        relayed[distance] = upper_coef
    far_node = jnp.zeros((probe_count, skeleton), jnp.float32)
    for offset in range(-COUPLE_REACH, COUPLE_REACH + 1):
        if abs(offset) < 2:
            continue
        partner = node_index + offset
        usable = (
            (partner >= 0) & (partner < node_total) & (node_coupling[0, offset + COUPLE_REACH] > 0)
        )
        clamped = jnp.clip(partner, 0, node_total - 1)
        partner_coef = relayed[offset]
        partner_points = lax.dynamic_index_in_dim(node_skeleton, clamped, 0, keepdims=False)
        kernel_tile = matern(partner_points, own_node, signal_variance)
        contribution = jnp.dot(partner_coef, kernel_tile, preferred_element_type=jnp.float32)
        far_node = far_node + jnp.where(usable, contribution, jnp.float32(0.0))
    pushed = lax.dot_general(
        group_local, group_transfer[0], (((1,), (1,)), ((), ())), preferred_element_type=jnp.float32
    )
    node_local = (pushed + far_node).astype(jnp.bfloat16)
    spread = lax.dot_general(
        node_local, transfer_flat, (((1,), (1,)), ((), ())), preferred_element_type=jnp.float32
    )
    leaf_local = (
        spread.reshape(probe_count, leaf_count, skeleton).transpose(1, 0, 2).astype(jnp.bfloat16)
    )
    far_leaf = lax.dot_general(
        leaf_local, leaf_basis, (((2,), (2,)), ((0,), (0,))), preferred_element_type=jnp.float32
    )
    result = far_leaf + near + noise_variance * ordered.astype(jnp.float32)
    restored = jax.vmap(restore_leaf)(result, leaf_order)
    return restored.astype(jnp.bfloat16)


def solution(mesh):
    finer = Mesh(mesh.devices.reshape(mesh.shape["group"], 4, 16), ("group", "dev_0", "dev_1"))
    return jax.shard_map(
        on_device,
        mesh=finer,
        in_specs=(
            P(GROUP_DEV, None, None),
            P(GROUP_DEV, None, None),
            P(GROUP_DEV, None),
            P(GROUP_DEV, None, None),
            P(GROUP_DEV, None, None, None),
            P(GROUP_DEV, None, None),
            P("group", None, None),
            P(),
            P(GROUP_DEV, None),
            P(GROUP_DEV, None),
            P(),
            P(),
        ),
        out_specs=P(GROUP_DEV, None, None),
        check_vma=False,
    )
```

profile of v0, /device:TPU:14, one launch (start us, length us, event | category | flops | bytes accessed | tf_op | source)
XLA Modules:
  0.0 357.8 jit_solution(2618776967792830066)
XLA Ops:
  0.0 0.9 compare_and_fusion
  0.9 0.7 or_bitcast_fusion
  1.6 1.4 copy.37
  3.1 40.2 %gather_fusion = bf16[4096,32]{1,0:T(8,128)(2,1)} fusion(bf16[4,32,1024]{1,2,0:T(8,128)(2,1)S(1)} %copy.37, s32[4096]{0:T(1024)S(1)} %bitcast.232), kind=kCustom, calls=%fused_computation | custom fusion | bytes 557056 | tf_op jit(solution)/shard_map/jit(take_along_axis)/gather | solution.py:95
  43.2 1.6 copy.39
  45.6 11.3 %collective-permute-start.4 = (bf16[32,256]{1,0:T(8,128)(2,1)S(1)}, bf16[32,256]{1,0:T(8,128)(2,1)}, u32[]{:S(2)}, u32[]{:S(2)}) collective-permute-start(bf16[32,256]{1,0:T(8,128)(2,1)S(1)} %convolution_convert_fusion.2), channel_id=1, source_target_pairs={{1,0},{2,1},{3,2},{4,3},{5,4},{6,5},{7,6},{8,7},{9,8},{10,9},{11,1... | collective-permute-start | bytes 49160 | tf_op jit(solution)/shard_map/ppermute | solution.py:63
  56.9 1.9 collective-permute-start
  58.9 1.9 collective-permute-start.10
  60.8 6.0 %collective-permute-start.11 = (f32[2,3,1024]{2,1,0:T(4,128)S(1)}, f32[2,3,1024]{2,1,0:T(4,128)}, u32[]{:S(2)}, u32[]{:S(2)}) collective-permute-start(f32[2,3,1024]{2,1,0:T(4,128)S(1)} %get-tuple-element.156), channel_id=1, source_target_pairs={{1,0},{2,1},{3,2},{4,3},{5,4},{6,5},{7,6},{8,7},{9,8},{10,9},{11,1... | collective-permute-start | bytes 73736 | tf_op jit(solution)/shard_map/ppermute | solution.py:28
  67.0 14.6 %psum.14 = f32[32,256]{1,0:T(8,128)S(1)} all-reduce(f32[32,256]{1,0:T(8,128)S(1)} %fusion.67), channel_id=1, replica_groups=mesh['group'=8,'dev_0'=4,'dev_1'=16] {'dev_0'}, use_global_device_ids=true, to_apply=%region_0.0 | all-reduce | flops 8192 | bytes 65536 | tf_op jit(solution)/shard_map/psum | solution.py:40
  81.6 54.2 %psum.15 = bf16[32,256]{1,0:T(8,128)(2,1)S(1)} all-reduce(f32[32,256]{1,0:T(8,128)S(1)} %psum.14), channel_id=1, replica_groups=mesh['group'=8,'dev_0'=4,'dev_1'=16] {'dev_1'}, use_global_device_ids=true, to_apply=%region_1.2 | all-reduce | flops 8192 | bytes 49152 | tf_op jit(solution)/shard_map/psum | solution.py:40
  136.4 4.8 %all-to-all-start = ((bf16[8,1,32,256]{3,2,1,0:T(8,128)(2,1)}), bf16[8,1,32,256]{3,2,1,0:T(8,128)(2,1)}, u32[]{:S(2)}, u32[]{:S(2)}) async-start(bf16[8,1,32,256]{3,2,1,0:T(8,128)(2,1)} %broadcast_in_dim.44), calls=%async_computation | async-start | bytes 262144 | tf_op jit(solution)/shard_map/all_to_all | solution.py:51
  141.3 0.7 fusion.241
  142.0 1.9 collective-permute-start.8
  145.5 1.7 constant_dynamic-slice_fusion.20
  153.8 6.0 %collective-permute-start.9 = (bf16[2,32,1024]{2,1,0:T(8,128)(2,1)}, bf16[2,32,1024]{2,1,0:T(8,128)(2,1)}, u32[]{:S(2)}, u32[]{:S(2)}) collective-permute-start(bf16[2,32,1024]{2,1,0:T(8,128)(2,1)} %get-tuple-element.133), channel_id=1, source_target_pairs={{1,0},{2,1},{3,2},{4,3},{5,4},{6,5},{7,6},{8,7},{9,8},{10,9},{11,1... | collective-permute-start | bytes 393224 | tf_op jit(solution)/shard_map/ppermute | solution.py:28
  159.8 2.1 collective-permute-start.5
  162.0 3.7 %collective-permute-start.1 = (bf16[32,256]{1,0:T(8,128)(2,1)}, bf16[32,256]{1,0:T(8,128)(2,1)S(1)}, u32[]{:S(2)}, u32[]{:S(2)}) collective-permute-start(bf16[32,256]{1,0:T(8,128)(2,1)} %collective-permute-done), channel_id=1, source_target_pairs={{0,1},{1,2},{2,3},{3,4},{4,5},{5,6},{6,7},{7,8},{8,9},{9,10},{10,1... | collective-permute-start | bytes 49160 | tf_op jit(solution)/shard_map/ppermute | solution.py:63
  165.7 0.8 pad_maximum_fusion.1
  166.6 4.2 %collective-permute-start.6 = (bf16[32,256]{1,0:T(8,128)(2,1)S(1)}, bf16[32,256]{1,0:T(8,128)(2,1)S(1)}, u32[]{:S(2)}, u32[]{:S(2)}) collective-permute-start(bf16[32,256]{1,0:T(8,128)(2,1)S(1)} %collective-permute-done.5), channel_id=1, source_target_pairs={{1,0},{2,1},{3,2},{4,3},{5,4},{6,5},{7,6},{8,7},{9,8},{10,9},{11,1... | collective-permute-start | bytes 49160 | tf_op jit(solution)/shard_map/ppermute | solution.py:63
  170.8 1.9 collective-permute-start.2
  172.8 1.1 convolution_select_fusion.3
  173.8 1.1 convolution_select_fusion.2
  174.9 6.0 %collective-permute-start.7 = (bf16[32,256]{1,0:T(8,128)(2,1)S(1)}, bf16[32,256]{1,0:T(8,128)(2,1)}, u32[]{:S(2)}, u32[]{:S(2)}) collective-permute-start(bf16[32,256]{1,0:T(8,128)(2,1)S(1)} %collective-permute-done.6), channel_id=1, source_target_pairs={{1,0},{2,1},{3,2},{4,3},{5,4},{6,5},{7,6},{8,7},{9,8},{10,9},{11,1... | collective-permute-start | bytes 49160 | tf_op jit(solution)/shard_map/ppermute | solution.py:63
  181.0 1.9 collective-permute-start.3
  183.3 5.4 %collective-permute-done.3 = bf16[32,256]{1,0:T(8,128)(2,1)S(1)} collective-permute-done((bf16[32,256]{1,0:T(8,128)(2,1)S(1)}, bf16[32,256]{1,0:T(8,128)(2,1)S(1)}, u32[]{:S(2)}, u32[]{:S(2)}) %collective-permute-start.3) | collective-permute-done | bytes 16416 | tf_op jit(solution)/shard_map/ppermute | solution.py:63
  189.2 1.0 fusion.46
  190.2 1.1 convolution_select_fusion.13
  191.4 1.1 fusion.56
  192.5 1.1 fusion.55
  193.6 1.1 fusion.54
  194.8 1.1 fusion.53
  195.9 1.1 fusion.52
  197.1 1.7 fusion.51
  198.8 1.3 fusion.60
  200.1 1.2 fusion.59
  201.3 1.7 fusion.43
  203.0 1.8 pad_maximum_fusion
  204.8 134.7 %while.12 = (s32[]{:T(128)}, f32[4,32,1024]{2,1,0:T(8,128)}, s32[4]{0:T(128)S(1)}, bf16[8,32,1024]{2,1,0:T(8,128)(2,1)}, f32[]{:T(128)}, /*index=5*/f32[8,3,1024...) while((s32[]{:T(128)}, f32[4,32,1024]{2,1,0:T(8,128)}, ...), condition=%wide.region_3.4_spmd, body=%wide.region_2.3_spmd.sunk | while | flops 409239584 | bytes 3852951 | solution.py:113
  217.1 4.9 %fusion.276 = f32[32,1024]{1,0:T(8,128)S(1)} fusion(f32[1024]{0:T(1024)S(1)} %bitcast.251, f32[1024]{0:T(1024)S(1)} %bitcast.264, f32[1024]{0:T(1024)S(1)} %bitcast.240, f32[1024]{0:T(1024)S(1)} %bitcast.262, f32[1024]{0:T(1024)S(1)} %bitcast.245, f32[1024]{0:T(1024)S(1)} %bitcast.263, f32[]{:T(128)} %get-tuple-element.315, f32[]{:T(128)} %bitcast.218, ...), kind=kOutput, calls=%fused_computation.21.clone.1 | convolution fusion | flops 81821696 | bytes 222212 | tf_op jit(solution)/shard_map/while/body/eval_jaxpr/dot_general | solution.py:107
  222.0 3.9 %fusion.275 = f32[32,1024]{1,0:T(8,128)S(1)} fusion(f32[1024]{0:T(1024)S(1)} %bitcast.252, f32[1024]{0:T(1024)S(1)} %bitcast.241, f32[1024]{0:T(1024)S(1)} %bitcast.246, f32[]{:T(128)} %get-tuple-element.315, f32[]{:T(128)} %bitcast.214, bf16[8,32,1024]{2,1,0:T(8,128)(2,1)S(1)} %copy-done.3, s32[]{:T(128)S(6)} %select_n.267), kind=kOutput, calls=%fused_computation.22.clone.1 | convolution fusion | flops 81821696 | bytes 221196 | tf_op jit(solution)/shard_map/while/body/eval_jaxpr/dot_general | solution.py:107
  225.9 4.0 %fusion.277 = f32[32,1024]{1,0:T(8,128)S(1)} fusion(f32[32,1024]{1,0:T(8,128)S(1)} %fusion.275, f32[32,1024]{1,0:T(8,128)S(1)} %fusion.276, f32[1024]{0:T(1024)S(1)} %bitcast.261, f32[1024]{0:T(1024)S(1)} %bitcast.259, f32[1024]{0:T(1024)S(1)} %bitcast.260, f32[1024]{0:T(1024)S(1)} %bitcast.253, f32[1024]{0:T(1024)S(1)} %bitcast.242, ...), kind=kOutput, calls=%fused_computation.20.clone.1 | convolution fusion | flops 81887232 | bytes 483340 | tf_op jit(solution)/shard_map/while/body/eval_jaxpr/dot_general | solution.py:107
  229.9 4.0 %fusion.278 = f32[32,1024]{1,0:T(8,128)S(1)} fusion(f32[32,1024]{1,0:T(8,128)S(1)} %fusion.277, f32[1024]{0:T(1024)S(1)} %bitcast.258, f32[1024]{0:T(1024)S(1)} %bitcast.256, f32[1024]{0:T(1024)S(1)} %bitcast.257, f32[1024]{0:T(1024)S(1)} %bitcast.254, f32[1024]{0:T(1024)S(1)} %bitcast.243, f32[1024]{0:T(1024)S(1)} %bitcast.248, ...), kind=kOutput, calls=%fused_computation.17.clone.1 | convolution fusion | flops 81854464 | bytes 352268 | tf_op jit(solution)/shard_map/while/body/eval_jaxpr/dot_general | solution.py:107
  233.9 4.6 %fusion.279 = f32[4,32,1024]{2,1,0:T(8,128)} fusion(f32[4,32,1024]{2,1,0:T(8,128)} %get-tuple-element.293, s32[]{:T(128)S(6)} %copy.62, f32[32,1024]{1,0:T(8,128)S(1)} %fusion.278, f32[1024]{0:T(1024)S(1)} %bitcast.250, f32[1024]{0:T(1024)S(1)} %bitcast.239, f32[1024]{0:T(1024)S(1)} %bitcast.238, f32[1024]{0:T(1024)S(1)} %bitcast.255, ...), kind=kOutput, calls=%fused_computation.15.clone.1 | convolution fusion | flops 81854464 | bytes 353288 | tf_op jit(solution)/shard_map/while/body/eval_jaxpr/dot_general | solution.py:107
  250.8 4.9 %fusion.276 = f32[32,1024]{1,0:T(8,128)S(1)} fusion(f32[1024]{0:T(1024)S(1)} %bitcast.251, f32[1024]{0:T(1024)S(1)} %bitcast.264, f32[1024]{0:T(1024)S(1)} %bitcast.240, f32[1024]{0:T(1024)S(1)} %bitcast.262, f32[1024]{0:T(1024)S(1)} %bitcast.245, f32[1024]{0:T(1024)S(1)} %bitcast.263, f32[]{:T(128)} %get-tuple-element.315, f32[]{:T(128)} %bitcast.218, ...), kind=kOutput, calls=%fused_computation.21.clone.1 | convolution fusion | flops 81821696 | bytes 222212 | tf_op jit(solution)/shard_map/while/body/eval_jaxpr/dot_general | solution.py:107
  255.7 3.9 %fusion.275 = f32[32,1024]{1,0:T(8,128)S(1)} fusion(f32[1024]{0:T(1024)S(1)} %bitcast.252, f32[1024]{0:T(1024)S(1)} %bitcast.241, f32[1024]{0:T(1024)S(1)} %bitcast.246, f32[]{:T(128)} %get-tuple-element.315, f32[]{:T(128)} %bitcast.214, bf16[8,32,1024]{2,1,0:T(8,128)(2,1)S(1)} %copy-done.3, s32[]{:T(128)S(6)} %select_n.267), kind=kOutput, calls=%fused_computation.22.clone.1 | convolution fusion | flops 81821696 | bytes 221196 | tf_op jit(solution)/shard_map/while/body/eval_jaxpr/dot_general | solution.py:107
  259.6 4.0 %fusion.277 = f32[32,1024]{1,0:T(8,128)S(1)} fusion(f32[32,1024]{1,0:T(8,128)S(1)} %fusion.275, f32[32,1024]{1,0:T(8,128)S(1)} %fusion.276, f32[1024]{0:T(1024)S(1)} %bitcast.261, f32[1024]{0:T(1024)S(1)} %bitcast.259, f32[1024]{0:T(1024)S(1)} %bitcast.260, f32[1024]{0:T(1024)S(1)} %bitcast.253, f32[1024]{0:T(1024)S(1)} %bitcast.242, ...), kind=kOutput, calls=%fused_computation.20.clone.1 | convolution fusion | flops 81887232 | bytes 483340 | tf_op jit(solution)/shard_map/while/body/eval_jaxpr/dot_general | solution.py:107
  263.6 4.0 %fusion.278 = f32[32,1024]{1,0:T(8,128)S(1)} fusion(f32[32,1024]{1,0:T(8,128)S(1)} %fusion.277, f32[1024]{0:T(1024)S(1)} %bitcast.258, f32[1024]{0:T(1024)S(1)} %bitcast.256, f32[1024]{0:T(1024)S(1)} %bitcast.257, f32[1024]{0:T(1024)S(1)} %bitcast.254, f32[1024]{0:T(1024)S(1)} %bitcast.243, f32[1024]{0:T(1024)S(1)} %bitcast.248, ...), kind=kOutput, calls=%fused_computation.17.clone.1 | convolution fusion | flops 81854464 | bytes 352268 | tf_op jit(solution)/shard_map/while/body/eval_jaxpr/dot_general | solution.py:107
  267.5 4.6 %fusion.279 = f32[4,32,1024]{2,1,0:T(8,128)} fusion(f32[4,32,1024]{2,1,0:T(8,128)} %get-tuple-element.293, s32[]{:T(128)S(6)} %copy.62, f32[32,1024]{1,0:T(8,128)S(1)} %fusion.278, f32[1024]{0:T(1024)S(1)} %bitcast.250, f32[1024]{0:T(1024)S(1)} %bitcast.239, f32[1024]{0:T(1024)S(1)} %bitcast.238, f32[1024]{0:T(1024)S(1)} %bitcast.255, ...), kind=kOutput, calls=%fused_computation.15.clone.1 | convolution fusion | flops 81854464 | bytes 353288 | tf_op jit(solution)/shard_map/while/body/eval_jaxpr/dot_general | solution.py:107
  284.5 4.9 %fusion.276 = f32[32,1024]{1,0:T(8,128)S(1)} fusion(f32[1024]{0:T(1024)S(1)} %bitcast.251, f32[1024]{0:T(1024)S(1)} %bitcast.264, f32[1024]{0:T(1024)S(1)} %bitcast.240, f32[1024]{0:T(1024)S(1)} %bitcast.262, f32[1024]{0:T(1024)S(1)} %bitcast.245, f32[1024]{0:T(1024)S(1)} %bitcast.263, f32[]{:T(128)} %get-tuple-element.315, f32[]{:T(128)} %bitcast.218, ...), kind=kOutput, calls=%fused_computation.21.clone.1 | convolution fusion | flops 81821696 | bytes 222212 | tf_op jit(solution)/shard_map/while/body/eval_jaxpr/dot_general | solution.py:107
  289.3 3.9 %fusion.275 = f32[32,1024]{1,0:T(8,128)S(1)} fusion(f32[1024]{0:T(1024)S(1)} %bitcast.252, f32[1024]{0:T(1024)S(1)} %bitcast.241, f32[1024]{0:T(1024)S(1)} %bitcast.246, f32[]{:T(128)} %get-tuple-element.315, f32[]{:T(128)} %bitcast.214, bf16[8,32,1024]{2,1,0:T(8,128)(2,1)S(1)} %copy-done.3, s32[]{:T(128)S(6)} %select_n.267), kind=kOutput, calls=%fused_computation.22.clone.1 | convolution fusion | flops 81821696 | bytes 221196 | tf_op jit(solution)/shard_map/while/body/eval_jaxpr/dot_general | solution.py:107
  293.3 4.0 %fusion.277 = f32[32,1024]{1,0:T(8,128)S(1)} fusion(f32[32,1024]{1,0:T(8,128)S(1)} %fusion.275, f32[32,1024]{1,0:T(8,128)S(1)} %fusion.276, f32[1024]{0:T(1024)S(1)} %bitcast.261, f32[1024]{0:T(1024)S(1)} %bitcast.259, f32[1024]{0:T(1024)S(1)} %bitcast.260, f32[1024]{0:T(1024)S(1)} %bitcast.253, f32[1024]{0:T(1024)S(1)} %bitcast.242, ...), kind=kOutput, calls=%fused_computation.20.clone.1 | convolution fusion | flops 81887232 | bytes 483340 | tf_op jit(solution)/shard_map/while/body/eval_jaxpr/dot_general | solution.py:107
  297.2 4.0 %fusion.278 = f32[32,1024]{1,0:T(8,128)S(1)} fusion(f32[32,1024]{1,0:T(8,128)S(1)} %fusion.277, f32[1024]{0:T(1024)S(1)} %bitcast.258, f32[1024]{0:T(1024)S(1)} %bitcast.256, f32[1024]{0:T(1024)S(1)} %bitcast.257, f32[1024]{0:T(1024)S(1)} %bitcast.254, f32[1024]{0:T(1024)S(1)} %bitcast.243, f32[1024]{0:T(1024)S(1)} %bitcast.248, ...), kind=kOutput, calls=%fused_computation.17.clone.1 | convolution fusion | flops 81854464 | bytes 352268 | tf_op jit(solution)/shard_map/while/body/eval_jaxpr/dot_general | solution.py:107
  301.2 4.6 %fusion.279 = f32[4,32,1024]{2,1,0:T(8,128)} fusion(f32[4,32,1024]{2,1,0:T(8,128)} %get-tuple-element.293, s32[]{:T(128)S(6)} %copy.62, f32[32,1024]{1,0:T(8,128)S(1)} %fusion.278, f32[1024]{0:T(1024)S(1)} %bitcast.250, f32[1024]{0:T(1024)S(1)} %bitcast.239, f32[1024]{0:T(1024)S(1)} %bitcast.238, f32[1024]{0:T(1024)S(1)} %bitcast.255, ...), kind=kOutput, calls=%fused_computation.15.clone.1 | convolution fusion | flops 81854464 | bytes 353288 | tf_op jit(solution)/shard_map/while/body/eval_jaxpr/dot_general | solution.py:107
  318.1 4.9 %fusion.276 = f32[32,1024]{1,0:T(8,128)S(1)} fusion(f32[1024]{0:T(1024)S(1)} %bitcast.251, f32[1024]{0:T(1024)S(1)} %bitcast.264, f32[1024]{0:T(1024)S(1)} %bitcast.240, f32[1024]{0:T(1024)S(1)} %bitcast.262, f32[1024]{0:T(1024)S(1)} %bitcast.245, f32[1024]{0:T(1024)S(1)} %bitcast.263, f32[]{:T(128)} %get-tuple-element.315, f32[]{:T(128)} %bitcast.218, ...), kind=kOutput, calls=%fused_computation.21.clone.1 | convolution fusion | flops 81821696 | bytes 222212 | tf_op jit(solution)/shard_map/while/body/eval_jaxpr/dot_general | solution.py:107
  323.0 3.9 %fusion.275 = f32[32,1024]{1,0:T(8,128)S(1)} fusion(f32[1024]{0:T(1024)S(1)} %bitcast.252, f32[1024]{0:T(1024)S(1)} %bitcast.241, f32[1024]{0:T(1024)S(1)} %bitcast.246, f32[]{:T(128)} %get-tuple-element.315, f32[]{:T(128)} %bitcast.214, bf16[8,32,1024]{2,1,0:T(8,128)(2,1)S(1)} %copy-done.3, s32[]{:T(128)S(6)} %select_n.267), kind=kOutput, calls=%fused_computation.22.clone.1 | convolution fusion | flops 81821696 | bytes 221196 | tf_op jit(solution)/shard_map/while/body/eval_jaxpr/dot_general | solution.py:107
  326.9 4.0 %fusion.277 = f32[32,1024]{1,0:T(8,128)S(1)} fusion(f32[32,1024]{1,0:T(8,128)S(1)} %fusion.275, f32[32,1024]{1,0:T(8,128)S(1)} %fusion.276, f32[1024]{0:T(1024)S(1)} %bitcast.261, f32[1024]{0:T(1024)S(1)} %bitcast.259, f32[1024]{0:T(1024)S(1)} %bitcast.260, f32[1024]{0:T(1024)S(1)} %bitcast.253, f32[1024]{0:T(1024)S(1)} %bitcast.242, ...), kind=kOutput, calls=%fused_computation.20.clone.1 | convolution fusion | flops 81887232 | bytes 483340 | tf_op jit(solution)/shard_map/while/body/eval_jaxpr/dot_general | solution.py:107
  330.9 4.0 %fusion.278 = f32[32,1024]{1,0:T(8,128)S(1)} fusion(f32[32,1024]{1,0:T(8,128)S(1)} %fusion.277, f32[1024]{0:T(1024)S(1)} %bitcast.258, f32[1024]{0:T(1024)S(1)} %bitcast.256, f32[1024]{0:T(1024)S(1)} %bitcast.257, f32[1024]{0:T(1024)S(1)} %bitcast.254, f32[1024]{0:T(1024)S(1)} %bitcast.243, f32[1024]{0:T(1024)S(1)} %bitcast.248, ...), kind=kOutput, calls=%fused_computation.17.clone.1 | convolution fusion | flops 81854464 | bytes 352268 | tf_op jit(solution)/shard_map/while/body/eval_jaxpr/dot_general | solution.py:107
  334.9 4.6 %fusion.279 = f32[4,32,1024]{2,1,0:T(8,128)} fusion(f32[4,32,1024]{2,1,0:T(8,128)} %get-tuple-element.293, s32[]{:T(128)S(6)} %copy.62, f32[32,1024]{1,0:T(8,128)S(1)} %fusion.278, f32[1024]{0:T(1024)S(1)} %bitcast.250, f32[1024]{0:T(1024)S(1)} %bitcast.239, f32[1024]{0:T(1024)S(1)} %bitcast.238, f32[1024]{0:T(1024)S(1)} %bitcast.255, ...), kind=kOutput, calls=%fused_computation.15.clone.1 | convolution fusion | flops 81854464 | bytes 353288 | tf_op jit(solution)/shard_map/while/body/eval_jaxpr/dot_general | solution.py:107
  339.5 1.2 add_bitcast_fusion
  340.6 2.0 copy.50
  342.6 12.3 %scatter_custom_fusion = f32[4096,32]{1,0:T(8,128)} fusion(s32[4096]{0:T(1024)} %bitcast.265, f32[4096,32]{1,0:T(8,128)} %bitcast.233, f32[]{:T(128)} %constant.160.clone.1), kind=kCustom, calls=%fused_computation.101 | custom fusion | bytes 524800
  355.0 1.9 copy.46
  357.0 0.8 copy.47
  (157 shorter events, 13.6 us)
Async XLA Ops:
  0.0 44.9 %copy-start = (bf16[4,1024,256]{2,1,0:T(8,128)(2,1)S(1)}, bf16[4,1024,256]{2,1,0:T(8,128)(2,1)}, u32[]{:S(2)}) copy-start(bf16[4,1024,256]{2,1,0:T(8,128)(2,1)} %param.17) | copy-start | bytes 6291460
  43.2 15.6 %copy-start.6 = (f32[4,3,1024]{2,0,1:T(4,128)S(1)}, f32[4,3,1024]{2,0,1:T(4,128)}, u32[]{:S(2)}) copy-start(f32[4,3,1024]{2,0,1:T(4,128)} %param.15) | copy-start | bytes 147460
  43.2 23.6 %copy-start.5 = (bf16[1,256,256]{2,1,0:T(8,128)(2,1)S(1)}, bf16[1,256,256]{2,1,0:T(8,128)(2,1)}, u32[]{:S(2)}) copy-start(bf16[1,256,256]{2,1,0:T(8,128)(2,1)} %param.19) | copy-start | bytes 393220
  44.9 99.1 %copy-start.4 = (s32[4,1024]{1,0:T(4,128)S(1)}, s32[4,1024]{1,0:T(4,128)}, u32[]{:S(2)}) copy-start(s32[4,1024]{1,0:T(4,128)} %param.16) | copy-start | bytes 49156
  44.9 99.1 %copy-start.49 = (s32[2]{0:T(128)S(1)}, s32[2]{0:T(128)}, u32[]{:S(2)}) copy-start(s32[2]{0:T(128)} %constant.198) | copy-start | bytes 28
  44.9 99.2 %copy-start.48 = (s32[2]{0:T(128)S(1)}, s32[2]{0:T(128)}, u32[]{:S(2)}) copy-start(s32[2]{0:T(128)} %constant.195) | copy-start | bytes 28
  44.9 99.3 %copy-start.8 = (f32[8,3,256]{2,0,1:T(8,128)S(1)}, f32[8,3,256]{2,0,1:T(8,128)}, u32[]{:S(2)}) copy-start(f32[8,3,256]{2,0,1:T(8,128)} %param.21) | copy-start | bytes 73732
  45.4 101.8 %copy-start.9 = (s32[1,9]{1,0:T(1,128)S(1)}, s32[1,9]{1,0:T(1,128)}, u32[]{:S(2)}) copy-start(s32[1,9]{1,0:T(1,128)} %param.23) | copy-start | bytes 112
  45.6 108.2 %collective-permute-start.4 = (bf16[32,256]{1,0:T(8,128)(2,1)S(1)}, bf16[32,256]{1,0:T(8,128)(2,1)}, u32[]{:S(2)}, u32[]{:S(2)}) collective-permute-start(bf16[32,256]{1,0:T(8,128)(2,1)S(1)} %convolution_convert_fusion.2), channel_id=1, source_target_pairs={{1,0},{2,1},{3,2},{4,3},{5,4},{6,5},{7,6},{8,7},{9,8},{10,9},{11,1... | collective-permute-start | bytes 49160 | tf_op jit(solution)/shard_map/ppermute | solution.py:63
  56.9 102.9 %collective-permute-start = (bf16[32,256]{1,0:T(8,128)(2,1)S(1)}, bf16[32,256]{1,0:T(8,128)(2,1)}, u32[]{:S(2)}, u32[]{:S(2)}) collective-permute-start(bf16[32,256]{1,0:T(8,128)(2,1)S(1)} %convolution_convert_fusion.2), channel_id=1, source_target_pairs={{0,1},{1,2},{2,3},{3,4},{4,5},{5,6},{6,7},{7,8},{8,9},{9,10},{10,1... | collective-permute-start | bytes 49160 | tf_op jit(solution)/shard_map/ppermute | solution.py:63
  58.9 103.1 %collective-permute-start.10 = (f32[2,3,1024]{2,1,0:T(4,128)S(1)}, f32[2,3,1024]{2,1,0:T(4,128)S(1)}, u32[]{:S(2)}, u32[]{:S(2)}) collective-permute-start(f32[2,3,1024]{2,1,0:T(4,128)S(1)} %get-tuple-element.155), channel_id=1, source_target_pairs={{0,1},{1,2},{2,3},{3,4},{4,5},{5,6},{6,7},{7,8},{8,9},{9,10},{10,1... | collective-permute-start | bytes 73736 | tf_op jit(solution)/shard_map/ppermute | solution.py:27
  60.8 104.9 %collective-permute-start.11 = (f32[2,3,1024]{2,1,0:T(4,128)S(1)}, f32[2,3,1024]{2,1,0:T(4,128)}, u32[]{:S(2)}, u32[]{:S(2)}) collective-permute-start(f32[2,3,1024]{2,1,0:T(4,128)S(1)} %get-tuple-element.156), channel_id=1, source_target_pairs={{1,0},{2,1},{3,2},{4,3},{5,4},{6,5},{7,6},{8,7},{9,8},{10,9},{11,1... | collective-permute-start | bytes 73736 | tf_op jit(solution)/shard_map/ppermute | solution.py:28
  136.4 53.8 %all-to-all-start = ((bf16[8,1,32,256]{3,2,1,0:T(8,128)(2,1)}), bf16[8,1,32,256]{3,2,1,0:T(8,128)(2,1)}, u32[]{:S(2)}, u32[]{:S(2)}) async-start(bf16[8,1,32,256]{3,2,1,0:T(8,128)(2,1)} %broadcast_in_dim.44), calls=%async_computation | async-start | bytes 262144 | tf_op jit(solution)/shard_map/all_to_all | solution.py:51
  142.0 61.0 %collective-permute-start.8 = (bf16[2,32,1024]{2,1,0:T(8,128)(2,1)}, bf16[2,32,1024]{2,1,0:T(8,128)(2,1)}, u32[]{:S(2)}, u32[]{:S(2)}) collective-permute-start(bf16[2,32,1024]{2,1,0:T(8,128)(2,1)} %get-tuple-element.132), channel_id=1, source_target_pairs={{0,1},{1,2},{2,3},{3,4},{4,5},{5,6},{6,7},{7,8},{8,9},{9,10},{10,1... | collective-permute-start | bytes 393224 | tf_op jit(solution)/shard_map/ppermute | solution.py:27
  147.1 42.0 %copy-start.20 = (f32[1,1,256]{2,0,1:T(1,128)}, f32[1,1,256]{2,0,1:T(1,128)S(1)}, u32[]{:S(2)}) copy-start(f32[1,1,256]{2,0,1:T(1,128)S(1)} %get-tuple-element.144) | copy-start | bytes 3076
  147.1 42.0 %copy-start.22 = (f32[1,1,256]{2,0,1:T(1,128)}, f32[1,1,256]{2,0,1:T(1,128)S(1)}, u32[]{:S(2)}) copy-start(f32[1,1,256]{2,0,1:T(1,128)S(1)} %get-tuple-element.146) | copy-start | bytes 3076
  147.1 42.0 %copy-start.24 = (f32[1,1,256]{2,0,1:T(1,128)}, f32[1,1,256]{2,0,1:T(1,128)S(1)}, u32[]{:S(2)}) copy-start(f32[1,1,256]{2,0,1:T(1,128)S(1)} %get-tuple-element.151) | copy-start | bytes 3076
  153.7 29.2 %copy-start.45 = (f32[1,1,256]{2,0,1:T(1,128)S(1)}, f32[1,1,256]{2,0,1:T(1,128)}, u32[]{:S(2)}) copy-start(f32[1,1,256]{2,0,1:T(1,128)} %get-tuple-element.142) | copy-start | bytes 3076
  153.7 35.0 %copy-start.42 = (f32[1,1,256]{2,0,1:T(1,128)S(1)}, f32[1,1,256]{2,0,1:T(1,128)}, u32[]{:S(2)}) copy-start(f32[1,1,256]{2,0,1:T(1,128)} %get-tuple-element.145) | copy-start | bytes 3076
  153.7 35.0 %copy-start.43 = (f32[1,1,256]{2,0,1:T(1,128)S(1)}, f32[1,1,256]{2,0,1:T(1,128)}, u32[]{:S(2)}) copy-start(f32[1,1,256]{2,0,1:T(1,128)} %get-tuple-element.147) | copy-start | bytes 3076
  153.7 35.0 %copy-start.44 = (f32[1,1,256]{2,0,1:T(1,128)S(1)}, f32[1,1,256]{2,0,1:T(1,128)}, u32[]{:S(2)}) copy-start(f32[1,1,256]{2,0,1:T(1,128)} %get-tuple-element.152) | copy-start | bytes 3076
  153.7 29.2 %copy-start.46 = (f32[1,1,256]{2,0,1:T(1,128)S(1)}, f32[1,1,256]{2,0,1:T(1,128)}, u32[]{:S(2)}) copy-start(f32[1,1,256]{2,0,1:T(1,128)} %get-tuple-element.143) | copy-start | bytes 3076
  153.7 29.2 %copy-start.47 = (f32[1,1,256]{2,0,1:T(1,128)S(1)}, f32[1,1,256]{2,0,1:T(1,128)}, u32[]{:S(2)}) copy-start(f32[1,1,256]{2,0,1:T(1,128)} %get-tuple-element.150) | copy-start | bytes 3076
  153.8 49.2 %collective-permute-start.9 = (bf16[2,32,1024]{2,1,0:T(8,128)(2,1)}, bf16[2,32,1024]{2,1,0:T(8,128)(2,1)}, u32[]{:S(2)}, u32[]{:S(2)}) collective-permute-start(bf16[2,32,1024]{2,1,0:T(8,128)(2,1)} %get-tuple-element.133), channel_id=1, source_target_pairs={{1,0},{2,1},{3,2},{4,3},{5,4},{6,5},{7,6},{8,7},{9,8},{10,9},{11,1... | collective-permute-start | bytes 393224 | tf_op jit(solution)/shard_map/ppermute | solution.py:28
  159.8 6.7 %collective-permute-start.5 = (bf16[32,256]{1,0:T(8,128)(2,1)}, bf16[32,256]{1,0:T(8,128)(2,1)S(1)}, u32[]{:S(2)}, u32[]{:S(2)}) collective-permute-start(bf16[32,256]{1,0:T(8,128)(2,1)} %collective-permute-done.4), channel_id=1, source_target_pairs={{1,0},{2,1},{3,2},{4,3},{5,4},{6,5},{7,6},{8,7},{9,8},{10,9},{11,1... | collective-permute-start | bytes 49160 | tf_op jit(solution)/shard_map/ppermute | solution.py:63
  162.0 8.8 %collective-permute-start.1 = (bf16[32,256]{1,0:T(8,128)(2,1)}, bf16[32,256]{1,0:T(8,128)(2,1)S(1)}, u32[]{:S(2)}, u32[]{:S(2)}) collective-permute-start(bf16[32,256]{1,0:T(8,128)(2,1)} %collective-permute-done), channel_id=1, source_target_pairs={{0,1},{1,2},{2,3},{3,4},{4,5},{5,6},{6,7},{7,8},{8,9},{9,10},{10,1... | collective-permute-start | bytes 49160 | tf_op jit(solution)/shard_map/ppermute | solution.py:63
  166.5 22.6 %copy-start.39 = (f32[1,1,256]{2,0,1:T(1,128)S(1)}, f32[1,1,256]{2,0,1:T(1,128)}, u32[]{:S(2)}) copy-start(f32[1,1,256]{2,0,1:T(1,128)} %get-tuple-element.136) | copy-start | bytes 3076
  166.5 22.6 %copy-start.40 = (f32[1,1,256]{2,0,1:T(1,128)S(1)}, f32[1,1,256]{2,0,1:T(1,128)}, u32[]{:S(2)}) copy-start(f32[1,1,256]{2,0,1:T(1,128)} %get-tuple-element.137) | copy-start | bytes 3076
  166.5 22.6 %copy-start.41 = (f32[1,1,256]{2,0,1:T(1,128)S(1)}, f32[1,1,256]{2,0,1:T(1,128)}, u32[]{:S(2)}) copy-start(f32[1,1,256]{2,0,1:T(1,128)} %get-tuple-element.154) | copy-start | bytes 3076
  166.6 8.3 %collective-permute-start.6 = (bf16[32,256]{1,0:T(8,128)(2,1)S(1)}, bf16[32,256]{1,0:T(8,128)(2,1)S(1)}, u32[]{:S(2)}, u32[]{:S(2)}) collective-permute-start(bf16[32,256]{1,0:T(8,128)(2,1)S(1)} %collective-permute-done.5), channel_id=1, source_target_pairs={{1,0},{2,1},{3,2},{4,3},{5,4},{6,5},{7,6},{8,7},{9,8},{10,9},{11,1... | collective-permute-start | bytes 49160 | tf_op jit(solution)/shard_map/ppermute | solution.py:63
  170.8 10.1 %collective-permute-start.2 = (bf16[32,256]{1,0:T(8,128)(2,1)S(1)}, bf16[32,256]{1,0:T(8,128)(2,1)S(1)}, u32[]{:S(2)}, u32[]{:S(2)}) collective-permute-start(bf16[32,256]{1,0:T(8,128)(2,1)S(1)} %collective-permute-done.1), channel_id=1, source_target_pairs={{0,1},{1,2},{2,3},{3,4},{4,5},{5,6},{6,7},{7,8},{8,9},{9,10},{10,1... | collective-permute-start | bytes 49160 | tf_op jit(solution)/shard_map/ppermute | solution.py:63
  173.8 16.4 %copy-start.36 = (f32[1,1,256]{2,0,1:T(1,128)S(1)}, f32[1,1,256]{2,0,1:T(1,128)}, u32[]{:S(2)}) copy-start(f32[1,1,256]{2,0,1:T(1,128)} %get-tuple-element.179) | copy-start | bytes 3076
  173.8 16.4 %copy-start.37 = (f32[1,1,256]{2,0,1:T(1,128)S(1)}, f32[1,1,256]{2,0,1:T(1,128)}, u32[]{:S(2)}) copy-start(f32[1,1,256]{2,0,1:T(1,128)} %get-tuple-element.180) | copy-start | bytes 3076
  173.8 16.4 %copy-start.38 = (f32[1,1,256]{2,0,1:T(1,128)S(1)}, f32[1,1,256]{2,0,1:T(1,128)}, u32[]{:S(2)}) copy-start(f32[1,1,256]{2,0,1:T(1,128)} %get-tuple-element.182) | copy-start | bytes 3076
  174.9 16.5 %copy-start.30 = (f32[1,1,256]{2,0,1:T(1,128)S(1)}, f32[1,1,256]{2,0,1:T(1,128)}, u32[]{:S(2)}) copy-start(f32[1,1,256]{2,0,1:T(1,128)} %get-tuple-element.176) | copy-start | bytes 3076
  174.9 16.5 %copy-start.31 = (f32[1,1,256]{2,0,1:T(1,128)S(1)}, f32[1,1,256]{2,0,1:T(1,128)}, u32[]{:S(2)}) copy-start(f32[1,1,256]{2,0,1:T(1,128)} %get-tuple-element.177) | copy-start | bytes 3076
  174.9 16.5 %copy-start.32 = (f32[1,1,256]{2,0,1:T(1,128)S(1)}, f32[1,1,256]{2,0,1:T(1,128)}, u32[]{:S(2)}) copy-start(f32[1,1,256]{2,0,1:T(1,128)} %get-tuple-element.178) | copy-start | bytes 3076
  174.9 25.2 %collective-permute-start.7 = (bf16[32,256]{1,0:T(8,128)(2,1)S(1)}, bf16[32,256]{1,0:T(8,128)(2,1)}, u32[]{:S(2)}, u32[]{:S(2)}) collective-permute-start(bf16[32,256]{1,0:T(8,128)(2,1)S(1)} %collective-permute-done.6), channel_id=1, source_target_pairs={{1,0},{2,1},{3,2},{4,3},{5,4},{6,5},{7,6},{8,7},{9,8},{10,9},{11,1... | collective-permute-start | bytes 49160 | tf_op jit(solution)/shard_map/ppermute | solution.py:63
  181.0 7.7 %collective-permute-start.3 = (bf16[32,256]{1,0:T(8,128)(2,1)S(1)}, bf16[32,256]{1,0:T(8,128)(2,1)S(1)}, u32[]{:S(2)}, u32[]{:S(2)}) collective-permute-start(bf16[32,256]{1,0:T(8,128)(2,1)S(1)} %collective-permute-done.2), channel_id=1, source_target_pairs={{0,1},{1,2},{2,3},{3,4},{4,5},{5,6},{6,7},{7,8},{8,9},{9,10},{10,1... | collective-permute-start | bytes 49160 | tf_op jit(solution)/shard_map/ppermute | solution.py:63
  183.3 9.2 %copy-start.33 = (f32[1,1,256]{2,0,1:T(1,128)S(1)}, f32[1,1,256]{2,0,1:T(1,128)}, u32[]{:S(2)}) copy-start(f32[1,1,256]{2,0,1:T(1,128)} %get-tuple-element.172) | copy-start | bytes 3076
  183.3 9.2 %copy-start.34 = (f32[1,1,256]{2,0,1:T(1,128)S(1)}, f32[1,1,256]{2,0,1:T(1,128)}, u32[]{:S(2)}) copy-start(f32[1,1,256]{2,0,1:T(1,128)} %get-tuple-element.173) | copy-start | bytes 3076
  183.3 9.2 %copy-start.35 = (f32[1,1,256]{2,0,1:T(1,128)S(1)}, f32[1,1,256]{2,0,1:T(1,128)}, u32[]{:S(2)}) copy-start(f32[1,1,256]{2,0,1:T(1,128)} %get-tuple-element.174) | copy-start | bytes 3076
  189.1 4.5 %copy-start.27 = (f32[1,1,256]{2,0,1:T(1,128)S(1)}, f32[1,1,256]{2,0,1:T(1,128)}, u32[]{:S(2)}) copy-start(f32[1,1,256]{2,0,1:T(1,128)} %get-tuple-element.169) | copy-start | bytes 3076
  189.1 4.5 %copy-start.28 = (f32[1,1,256]{2,0,1:T(1,128)S(1)}, f32[1,1,256]{2,0,1:T(1,128)}, u32[]{:S(2)}) copy-start(f32[1,1,256]{2,0,1:T(1,128)} %get-tuple-element.170) | copy-start | bytes 3076
  189.1 4.5 %copy-start.29 = (f32[1,1,256]{2,0,1:T(1,128)S(1)}, f32[1,1,256]{2,0,1:T(1,128)}, u32[]{:S(2)}) copy-start(f32[1,1,256]{2,0,1:T(1,128)} %get-tuple-element.171) | copy-start | bytes 3076
  190.2 4.6 %copy-start.15 = (f32[1,1,256]{2,0,1:T(1,128)S(1)}, f32[1,1,256]{2,0,1:T(1,128)}, u32[]{:S(2)}) copy-start(f32[1,1,256]{2,0,1:T(1,128)} %get-tuple-element.166) | copy-start | bytes 3076
  190.2 4.6 %copy-start.16 = (f32[1,1,256]{2,0,1:T(1,128)S(1)}, f32[1,1,256]{2,0,1:T(1,128)}, u32[]{:S(2)}) copy-start(f32[1,1,256]{2,0,1:T(1,128)} %get-tuple-element.167) | copy-start | bytes 3076
  190.2 4.6 %copy-start.17 = (f32[1,1,256]{2,0,1:T(1,128)S(1)}, f32[1,1,256]{2,0,1:T(1,128)}, u32[]{:S(2)}) copy-start(f32[1,1,256]{2,0,1:T(1,128)} %get-tuple-element.168) | copy-start | bytes 3076
  191.3 4.6 %copy-start.12 = (f32[1,1,256]{2,0,1:T(1,128)S(1)}, f32[1,1,256]{2,0,1:T(1,128)}, u32[]{:S(2)}) copy-start(f32[1,1,256]{2,0,1:T(1,128)} %get-tuple-element.163) | copy-start | bytes 3076
  191.3 4.6 %copy-start.13 = (f32[1,1,256]{2,0,1:T(1,128)S(1)}, f32[1,1,256]{2,0,1:T(1,128)}, u32[]{:S(2)}) copy-start(f32[1,1,256]{2,0,1:T(1,128)} %get-tuple-element.164) | copy-start | bytes 3076
  191.3 4.6 %copy-start.14 = (f32[1,1,256]{2,0,1:T(1,128)S(1)}, f32[1,1,256]{2,0,1:T(1,128)}, u32[]{:S(2)}) copy-start(f32[1,1,256]{2,0,1:T(1,128)} %get-tuple-element.165) | copy-start | bytes 3076
  192.5 4.6 %copy-start.10 = (f32[1,1,256]{2,0,1:T(1,128)S(1)}, f32[1,1,256]{2,0,1:T(1,128)}, u32[]{:S(2)}) copy-start(f32[1,1,256]{2,0,1:T(1,128)} %get-tuple-element.161) | copy-start | bytes 3076
  192.5 4.6 %copy-start.11 = (f32[1,1,256]{2,0,1:T(1,128)S(1)}, f32[1,1,256]{2,0,1:T(1,128)}, u32[]{:S(2)}) copy-start(f32[1,1,256]{2,0,1:T(1,128)} %get-tuple-element.162) | copy-start | bytes 3076
  194.8 5.3 %copy-start.18 = (f32[1,1,256]{2,0,1:T(1,128)S(1)}, f32[1,1,256]{2,0,1:T(1,128)}, u32[]{:S(2)}) copy-start(f32[1,1,256]{2,0,1:T(1,128)} %get-tuple-element.134) | copy-start | bytes 3076
  194.8 5.3 %copy-start.19 = (f32[1,1,256]{2,0,1:T(1,128)S(1)}, f32[1,1,256]{2,0,1:T(1,128)}, u32[]{:S(2)}) copy-start(f32[1,1,256]{2,0,1:T(1,128)} %get-tuple-element.135) | copy-start | bytes 3076
  194.8 5.3 %copy-start.21 = (f32[1,1,256]{2,0,1:T(1,128)S(1)}, f32[1,1,256]{2,0,1:T(1,128)}, u32[]{:S(2)}) copy-start(f32[1,1,256]{2,0,1:T(1,128)} %copy-done.20) | copy-start | bytes 3076
  194.8 5.3 %copy-start.23 = (f32[1,1,256]{2,0,1:T(1,128)S(1)}, f32[1,1,256]{2,0,1:T(1,128)}, u32[]{:S(2)}) copy-start(f32[1,1,256]{2,0,1:T(1,128)} %copy-done.22) | copy-start | bytes 3076
  194.8 5.3 %copy-start.25 = (f32[1,1,256]{2,0,1:T(1,128)S(1)}, f32[1,1,256]{2,0,1:T(1,128)}, u32[]{:S(2)}) copy-start(f32[1,1,256]{2,0,1:T(1,128)} %copy-done.24) | copy-start | bytes 3076
  194.8 5.3 %copy-start.26 = (f32[1,1,256]{2,0,1:T(1,128)S(1)}, f32[1,1,256]{2,0,1:T(1,128)}, u32[]{:S(2)}) copy-start(f32[1,1,256]{2,0,1:T(1,128)} %get-tuple-element.153) | copy-start | bytes 3076
  204.8 134.7 %copy-start.2 = (f32[4,32,1024]{2,1,0:T(8,128)S(1)}, f32[4,32,1024]{2,1,0:T(8,128)}, u32[]{:S(2)}) copy-start(f32[4,32,1024]{2,1,0:T(8,128)} %fusion.43) | copy-start | bytes 1572868
  217.1 4.9 %copy-start.3 = (bf16[8,32,1024]{2,1,0:T(8,128)(2,1)S(1)}, bf16[8,32,1024]{2,1,0:T(8,128)(2,1)}, u32[]{:S(2)}) copy-start(bf16[8,32,1024]{2,1,0:T(8,128)(2,1)} %get-tuple-element.314) | copy-start | bytes 1572868 | tf_op jit(solution)/shard_map/while
  250.8 4.9 %copy-start.3 = (bf16[8,32,1024]{2,1,0:T(8,128)(2,1)S(1)}, bf16[8,32,1024]{2,1,0:T(8,128)(2,1)}, u32[]{:S(2)}) copy-start(bf16[8,32,1024]{2,1,0:T(8,128)(2,1)} %get-tuple-element.314) | copy-start | bytes 1572868 | tf_op jit(solution)/shard_map/while
  284.5 4.9 %copy-start.3 = (bf16[8,32,1024]{2,1,0:T(8,128)(2,1)S(1)}, bf16[8,32,1024]{2,1,0:T(8,128)(2,1)}, u32[]{:S(2)}) copy-start(bf16[8,32,1024]{2,1,0:T(8,128)(2,1)} %get-tuple-element.314) | copy-start | bytes 1572868 | tf_op jit(solution)/shard_map/while
  318.1 4.9 %copy-start.3 = (bf16[8,32,1024]{2,1,0:T(8,128)(2,1)S(1)}, bf16[8,32,1024]{2,1,0:T(8,128)(2,1)}, u32[]{:S(2)}) copy-start(bf16[8,32,1024]{2,1,0:T(8,128)(2,1)} %get-tuple-element.314) | copy-start | bytes 1572868 | tf_op jit(solution)/shard_map/while
  (2 other events, 5.9 us)
where the time goes:
time: 360 us; the launch traced here: 358 us
  matrix products  102 us (28%)
  local copies, waits for them, and re-layouts  74.3 us (21%)
  blocking collectives  68.8 us (19%)
  starting transfers between devices  53.8 us (15%)
  loops' own time  41.3 us (11%)
  between operations  6.16 us (2%)
  other arithmetic  5.62 us (2%)
  waiting for transfers between devices  5.42 us (2%)
    dot_general x20, matrix products, near_leaf(): jnp.dot(values, kernel_tile, preferred_element_type=jnp.float32)  85.3 us
    psum x2, blocking collectives, by_axis(): return functools.reduce(lax.psum, axes, value)  68.8 us
    gather x2, local copies, waits for them, and re-layouts, on_device(): ordered = jnp.take_along_axis(probes, leaf_order[:, None, :], axis=2)  41.8 us
    another operation x1, loops' own time, on_device(): lax.map(near_leaf, (jnp.arange(leaf_count, dtype=jnp.int32), near_pattern))  41.3 us
    ppermute x8, starting transfers between devices, from_behind(): return lax.ppermute(block, axis, route)  33.2 us
    unnamed x104, local copies, waits for them, and re-layouts  16.5 us
    ppermute x2, starting transfers between devices, with_halo(): lax.ppermute(leading, axis, [(b, a) for a, b in up])  12.1 us
    dot_general x7, matrix products, on_device(): jnp.dot(group_coef[other], kernel_tile, preferred_element_type=jnp.float32)  8.34 us
  transfers between devices with their start and end apart: 13, of which 1 were waited for; matrix products, arithmetic and copies ran while one was open for 6% of the time, Pallas kernels for 0%

commit v1 on v0

v1 whole, which is shorter than its diff:
```python
import jax
import jax.numpy as jnp
from jax import lax
from jax.sharding import Mesh
from jax.sharding import PartitionSpec as P

NEAR_REACH = 2
COUPLE_REACH = 4
GROUP_DEV = ("group", "dev_0", "dev_1")
DEV = ("dev_0", "dev_1")


ROOT_THREE = 1.7320508075688772
LENGTH_SCALE = 0.5


def with_halo(value, axis, width):
    peers, length = (lax.axis_size(axis), value.shape[0])
    up = [(i, i + 1) for i in range(peers - 1)]
    last = value[length - width :]
    leading = value[:width]
    low = lax.ppermute(last, axis, up)
    high = lax.ppermute(leading, axis, [(b, a) for a, b in up])
    return jnp.concatenate([low, value, high], axis=0)


def from_behind(block, axis, distance):
    devices = range(lax.axis_size(axis))
    route = [(i - distance, i) for i in devices if i - distance in devices]
    return lax.ppermute(block, axis, route)


def matern(source, target, amplitude):
    square = (source[0][:, None] - target[0][None, :]) ** 2
    square = square + (source[1][:, None] - target[1][None, :]) ** 2
    square = square + (source[2][:, None] - target[2][None, :]) ** 2
    scaled = jnp.sqrt(square) * (ROOT_THREE / LENGTH_SCALE)
    return (amplitude * (1.0 + scaled) * jnp.exp(-scaled)).astype(jnp.bfloat16)


def one_hot(ordering, size):
    rows = lax.broadcasted_iota(jnp.int32, (size, size), 0)
    return (rows == ordering[None, :]).astype(jnp.bfloat16)


def on_device(
    probes,
    points,
    leaf_order,
    leaf_basis,
    node_transfer,
    group_transfer,
    node_skeleton,
    group_skeleton,
    near_pattern,
    node_coupling,
    signal_variance,
    noise_variance,
):
    leaf_count, probe_count, leaf_size = probes.shape
    skeleton = leaf_basis.shape[2]
    f32 = jnp.float32

    hots = [one_hot(leaf_order[i], leaf_size) for i in range(leaf_count)]
    ordered = jnp.stack(
        [
            jnp.dot(probes[i], hots[i], preferred_element_type=f32).astype(jnp.bfloat16)
            for i in range(leaf_count)
        ]
    )

    leaf_coef = lax.dot_general(
        ordered, leaf_basis, (((2,), (1,)), ((0,), (0,))), preferred_element_type=f32
    ).astype(jnp.bfloat16)
    stacked = leaf_coef.transpose(1, 0, 2).reshape(probe_count, leaf_count * skeleton)
    transfer_flat = node_transfer[0].reshape(leaf_count * skeleton, skeleton)
    node_coef = jnp.dot(stacked, transfer_flat, preferred_element_type=f32).astype(jnp.bfloat16)
    group_term = jnp.dot(node_coef, group_transfer[0], preferred_element_type=f32)
    own_coef = lax.psum(group_term, DEV).astype(jnp.bfloat16)
    group_coef = lax.all_gather(own_coef, "group", axis=0, tiled=False)

    node_index = lax.axis_index(DEV)
    node_total = lax.axis_size(DEV)
    relayed = {}
    for offset in range(-COUPLE_REACH, COUPLE_REACH + 1):
        if abs(offset) < 2:
            continue
        relayed[offset] = from_behind(node_coef, DEV, -offset)

    wide_probes = with_halo(ordered, GROUP_DEV, NEAR_REACH)
    wide_points = with_halo(points, GROUP_DEV, NEAR_REACH)
    wide = leaf_count + 2 * NEAR_REACH
    own = range(NEAR_REACH, NEAR_REACH + leaf_count)
    pattern = near_pattern.astype(f32)
    near = [jnp.zeros((probe_count, leaf_size), f32) for _ in range(leaf_count)]
    for b in own:
        tile = matern(wide_points[b], wide_points[b], signal_variance)
        t = b - NEAR_REACH
        near[t] = near[t] + jnp.dot(
            wide_probes[b], tile, preferred_element_type=f32
        ) * pattern[t, NEAR_REACH]
    for gap in range(1, NEAR_REACH + 1):
        for a in range(wide - gap):
            b = a + gap
            if a not in own and b not in own:
                continue
            tile = matern(wide_points[a], wide_points[b], signal_variance)
            if b in own:
                t = b - NEAR_REACH
                near[t] = near[t] + jnp.dot(
                    wide_probes[a], tile, preferred_element_type=f32
                ) * pattern[t, NEAR_REACH - gap]
            if a in own:
                t = a - NEAR_REACH
                near[t] = near[t] + lax.dot_general(
                    wide_probes[b], tile, (((1,), (1,)), ((), ())), preferred_element_type=f32
                ) * pattern[t, NEAR_REACH + gap]
    near = jnp.stack(near)

    group_index = lax.axis_index("group")
    group_total = lax.axis_size("group")
    own_skeleton = lax.dynamic_index_in_dim(group_skeleton, group_index, 0, keepdims=False)
    far_group = jnp.zeros((probe_count, skeleton), f32)
    for other in range(group_total):
        kernel_tile = matern(group_skeleton[other], own_skeleton, signal_variance)
        contribution = jnp.dot(group_coef[other], kernel_tile, preferred_element_type=f32)
        far_group = far_group + jnp.where(other != group_index, contribution, f32(0.0))
    group_local = far_group.astype(jnp.bfloat16)

    own_node = lax.dynamic_index_in_dim(node_skeleton, node_index, 0, keepdims=False)
    far_node = jnp.zeros((probe_count, skeleton), f32)
    for offset in range(-COUPLE_REACH, COUPLE_REACH + 1):
        if abs(offset) < 2:
            continue
        partner = node_index + offset
        usable = (
            (partner >= 0) & (partner < node_total) & (node_coupling[0, offset + COUPLE_REACH] > 0)
        )
        clamped = jnp.clip(partner, 0, node_total - 1)
        partner_points = lax.dynamic_index_in_dim(node_skeleton, clamped, 0, keepdims=False)
        kernel_tile = matern(partner_points, own_node, signal_variance)
        contribution = jnp.dot(relayed[offset], kernel_tile, preferred_element_type=f32)
        far_node = far_node + jnp.where(usable, contribution, f32(0.0))

    pushed = lax.dot_general(
        group_local, group_transfer[0], (((1,), (1,)), ((), ())), preferred_element_type=f32
    )
    node_local = (pushed + far_node).astype(jnp.bfloat16)
    spread = lax.dot_general(
        node_local, transfer_flat, (((1,), (1,)), ((), ())), preferred_element_type=f32
    )
    leaf_local = (
        spread.reshape(probe_count, leaf_count, skeleton).transpose(1, 0, 2).astype(jnp.bfloat16)
    )
    far_leaf = lax.dot_general(
        leaf_local, leaf_basis, (((2,), (2,)), ((0,), (0,))), preferred_element_type=f32
    )
    result = (far_leaf + near + noise_variance * ordered.astype(f32)).astype(jnp.bfloat16)
    restored = [
        lax.dot_general(
            result[i], hots[i], (((1,), (1,)), ((), ())), preferred_element_type=f32
        ).astype(jnp.bfloat16)
        for i in range(leaf_count)
    ]
    return jnp.stack(restored)


def solution(mesh):
    finer = Mesh(mesh.devices.reshape(mesh.shape["group"], 4, 16), ("group", "dev_0", "dev_1"))
    return jax.shard_map(
        on_device,
        mesh=finer,
        in_specs=(
            P(GROUP_DEV, None, None),
            P(GROUP_DEV, None, None),
            P(GROUP_DEV, None),
            P(GROUP_DEV, None, None),
            P(GROUP_DEV, None, None, None),
            P(GROUP_DEV, None, None),
            P("group", None, None),
            P(),
            P(GROUP_DEV, None),
            P(GROUP_DEV, None),
            P(),
            P(),
        ),
        out_specs=P(GROUP_DEV, None, None),
        check_vma=False,
    )
```

time: 360 us -> 460 us (1.28)
  the two profiles are of different devices: /device:TPU:14 before, /device:TPU:1 now
where the time goes in v1:
time: 460 us; the launch traced here: 453 us
  blocking collectives  296 us (64%)
  matrix products  112 us (24%)
  starting transfers between devices  31.9 us (7%)
  between operations  6 us (1%)
  local copies, waits for them, and re-layouts  5.95 us (1%)
    psum x1, blocking collectives, on_device(): own_coef = lax.psum(group_term, DEV).astype(jnp.bfloat16)  227 us
    all_gather x1, blocking collectives, on_device(): group_coef = lax.all_gather(own_coef, 'group', axis=0, tiled=False)  69.1 us
    dot_general x8, matrix products, on_device(): lax.dot_general(wide_probes[b], tile, (((1,), (1,)), ((), ())), preferred...  36 us
    dot_general x8, matrix products, on_device(): jnp.dot(wide_probes[a], tile, preferred_element_type=f32)  34.8 us
    ppermute x6, starting transfers between devices, from_behind(): return lax.ppermute(block, axis, route)  20.8 us
    dot_general x4, matrix products, on_device(): jnp.dot(wide_probes[b], tile, preferred_element_type=f32)  18.2 us
  transfers between devices with their start and end apart: 10, of which 0 were waited for; matrix products, arithmetic and copies ran while one was open for 18% of the time, Pallas kernels for 0%

profile of v1, /device:TPU:1, one launch (start us, length us, event | category | flops | bytes accessed | tf_op | source)
XLA Modules:
  0.0 452.6 jit_solution(511612065906438201)
XLA Ops:
  0.0 0.9 fusion.346
  1.0 1.6 fusion.84
  2.6 1.6 fusion.82
  4.2 0.8 fusion.80
  5.0 0.8 fusion.78
  5.9 0.4 fusion.90
  6.5 1.3 collective-permute-start.5
  7.8 1.3 collective-permute-start.4
  9.1 1.3 collective-permute-start.3
  10.4 6.9 %collective-permute-start.2 = (bf16[32,256]{1,0:T(8,128)(2,1)S(1)}, bf16[32,256]{1,0:T(8,128)(2,1)}, u32[]{:S(2)}, u32[]{:S(2)}) collective-permute-start(bf16[32,256]{1,0:T(8,128)(2,1)S(1)} %convolution_convert_fusion.2), channel_id=1, source_target_pairs={{0,2},{1,3},{2,4},{3,5},{4,6},{5,7},{6,8},{7,9},{8,10},{9,11},{10,... | collective-permute-start | bytes 49160 | tf_op jit(solution)/shard_map/ppermute | solution.py:30
  17.4 8.7 %collective-permute-start.1 = (bf16[32,256]{1,0:T(8,128)(2,1)S(1)}, bf16[32,256]{1,0:T(8,128)(2,1)}, u32[]{:S(2)}, u32[]{:S(2)}) collective-permute-start(bf16[32,256]{1,0:T(8,128)(2,1)S(1)} %convolution_convert_fusion.2), channel_id=1, source_target_pairs={{0,3},{1,4},{2,5},{3,6},{4,7},{5,8},{6,9},{7,10},{8,11},{9,12},{10... | collective-permute-start | bytes 49160 | tf_op jit(solution)/shard_map/ppermute | solution.py:30
  26.2 0.7 fusion.347
  27.0 0.6 slice.711
  27.5 0.6 fusion.345
  28.1 0.7 fusion.344
  29.6 226.5 %psum.7 = bf16[32,256]{1,0:T(8,128)(2,1)S(1)} all-reduce(f32[32,256]{1,0:T(8,128)S(1)} %fusion.112), channel_id=1, replica_groups=mesh['group'=8,'dev_0'=4,'dev_1'=16] {'dev_0','dev_1'}, use_global_device_ids=true, to_apply=%region_0.0 | all-reduce | flops 8192 | bytes 49152 | tf_op jit(solution)/shard_map/psum | solution.py:79
  256.2 69.1 %all-gather = bf16[256,256]{1,0:T(8,128)(2,1)S(1)} all-gather(bf16[32,256]{1,0:T(8,128)(2,1)S(1)} %psum.7), channel_id=2, replica_groups=mesh['group'=8,'dev_0'=4,'dev_1'=16] {'group'}, dimensions={0}, use_global_device_ids=true | all-gather | bytes 147456 | tf_op jit(solution)/shard_map/all_gather | solution.py:80
  325.2 4.6 %fusion.74 = f32[32,1024]{1,0:T(8,128)} fusion(bf16[1024,32]{0,1:T(8,128)(2,1)S(1)} %fusion.84, f32[1024]{0:T(1024)S(1)} %bitcast.263, f32[1024]{0:T(1024)S(1)} %bitcast.249, f32[1024]{0:T(1024)S(1)} %bitcast.256, f32[]{:T(128)S(6)} %copy.15, f32[]{:T(128)} %bitcast.122), kind=kOutput, calls=%fused_computation.94 | convolution fusion | flops 81821696 | bytes 208904 | tf_op jit(solution)/shard_map/dot_general | solution.py:99
  329.8 5.3 %fusion.43 = f32[32,1024]{1,0:T(8,128)} fusion(bf16[1024,32]{0,1:T(8,128)(2,1)S(1)} %fusion.84, f32[1024]{0:T(1024)S(1)} %bitcast.264, f32[1024]{0:T(1024)S(1)} %bitcast.250, f32[1024]{0:T(1024)S(1)} %bitcast.257, f32[1024]{0:T(1024)S(1)} %bitcast.270, f32[1024]{0:T(1024)S(1)} %bitcast.278, f32[1024]{0:T(1024)S(1)} %bitcast.286, f32[]{:T(128)S(6)} %copy.15, ...), kind=kOutput, calls=%fused_computation.63 | convolution fusion | flops 81821696 | bytes 221192 | tf_op jit(solution)/shard_map/dot_general | solution.py:115
  335.1 4.6 %fusion.76 = f32[32,1024]{1,0:T(8,128)} fusion(bf16[1024,32]{0,1:T(8,128)(2,1)S(1)} %fusion.80, f32[1024]{0:T(1024)S(1)} %bitcast.271, f32[1024]{0:T(1024)S(1)} %bitcast.279, f32[1024]{0:T(1024)S(1)} %bitcast.287, f32[]{:T(128)S(6)} %copy.15, f32[]{:T(128)} %bitcast.101), kind=kOutput, calls=%fused_computation.96 | convolution fusion | flops 81821696 | bytes 208904 | tf_op jit(solution)/shard_map/dot_general | solution.py:99
  339.7 4.5 %fusion.75 = f32[32,1024]{1,0:T(8,128)} fusion(bf16[1024,32]{0,1:T(8,128)(2,1)S(1)} %fusion.82, f32[1024]{0:T(1024)S(1)} %bitcast.294, f32[1024]{0:T(1024)S(1)} %bitcast.302, f32[1024]{0:T(1024)S(1)} %bitcast.310, f32[]{:T(128)S(6)} %copy.15, f32[]{:T(128)} %bitcast.110), kind=kOutput, calls=%fused_computation.95 | convolution fusion | flops 81821696 | bytes 208904 | tf_op jit(solution)/shard_map/dot_general | solution.py:99
  344.3 4.6 %fusion.51 = f32[32,1024]{1,0:T(8,128)} fusion(bf16[1024,32]{0,1:T(8,128)(2,1)S(1)} %fusion.78, f32[1024]{0:T(1024)S(1)} %bitcast.295, f32[1024]{0:T(1024)S(1)} %bitcast.303, f32[1024]{0:T(1024)S(1)} %bitcast.311, f32[1024]{0:T(1024)S(1)} %bitcast.235, f32[1024]{0:T(1024)S(1)} %bitcast.242, f32[1024]{0:T(1024)S(1)} %bitcast.228, f32[]{:T(128)S(6)} %copy.15, ...), kind=kOutput, calls=%fused_computation.71 | convolution fusion | flops 81821696 | bytes 221192 | tf_op jit(solution)/shard_map/dot_general | solution.py:110
  348.9 5.0 %fusion.50 = f32[32,1024]{1,0:T(8,128)} fusion(bf16[1024,32]{0,1:T(8,128)(2,1)S(1)} %fusion.82, f32[1024]{0:T(1024)S(1)} %bitcast.296, f32[1024]{0:T(1024)S(1)} %bitcast.304, f32[1024]{0:T(1024)S(1)} %bitcast.312, f32[1024]{0:T(1024)S(1)} %bitcast.236, f32[1024]{0:T(1024)S(1)} %bitcast.243, f32[1024]{0:T(1024)S(1)} %bitcast.229, f32[]{:T(128)S(6)} %copy.15, ...), kind=kOutput, calls=%fused_computation.70 | convolution fusion | flops 81821696 | bytes 221192 | tf_op jit(solution)/shard_map/dot_general | solution.py:115
  353.9 4.5 %fusion.77 = f32[32,1024]{1,0:T(8,128)} fusion(bf16[1024,32]{0,1:T(8,128)(2,1)S(1)} %fusion.78, f32[1024]{0:T(1024)S(1)} %bitcast.237, f32[1024]{0:T(1024)S(1)} %bitcast.244, f32[1024]{0:T(1024)S(1)} %bitcast.230, f32[]{:T(128)S(6)} %copy.15, f32[]{:T(128)} %bitcast.79), kind=kOutput, calls=%fused_computation.97 | convolution fusion | flops 81821696 | bytes 208904 | tf_op jit(solution)/shard_map/dot_general | solution.py:99
  358.4 5.5 %fusion.42 = f32[32,1024]{1,0:T(8,128)} fusion(f32[32,1024]{1,0:T(8,128)} %fusion.74, bf16[1024,32]{0,1:T(8,128)(2,1)S(1)} %fusion.82, f32[1024]{0:T(1024)S(1)} %bitcast.297, f32[1024]{0:T(1024)S(1)} %bitcast.305, f32[1024]{0:T(1024)S(1)} %bitcast.313, f32[1024]{0:T(1024)S(1)} %bitcast.265, f32[1024]{0:T(1024)S(1)} %bitcast.251, f32[1024]{0:T(1024)S(1)} %bitcast.258, ...), kind=kOutput, calls=%fused_computation.62 | convolution fusion | flops 81854464 | bytes 352264 | tf_op jit(solution)/shard_map/dot_general | solution.py:110
  364.0 3.9 fusion.49
  367.9 4.1 fusion.55
  372.1 4.9 %fusion.47 = f32[32,1024]{1,0:T(8,128)} fusion(f32[32,1024]{1,0:T(8,128)S(1)} %fusion.55, bf16[1024,32]{0,1:T(8,128)(2,1)S(1)} %fusion.82, f32[1024]{0:T(1024)S(1)} %bitcast.274, f32[1024]{0:T(1024)S(1)} %bitcast.282, f32[1024]{0:T(1024)S(1)} %bitcast.290, f32[1024]{0:T(1024)S(1)} %bitcast.299, f32[1024]{0:T(1024)S(1)} %bitcast.307, ...), kind=kOutput, calls=%fused_computation.67 | convolution fusion | flops 81854464 | bytes 352264 | tf_op jit(solution)/shard_map/dot_general | solution.py:115
  377.0 4.9 %fusion.40 = f32[32,1024]{1,0:T(8,128)} fusion(f32[32,1024]{1,0:T(8,128)S(1)} %copy-done.39, f32[32,1024]{1,0:T(8,128)S(1)} %fusion.49, bf16[1024,32]{0,1:T(8,128)(2,1)S(1)} %fusion.84, f32[1024]{0:T(1024)S(1)} %bitcast.300, f32[1024]{0:T(1024)S(1)} %bitcast.308, f32[1024]{0:T(1024)S(1)} %bitcast.316, f32[1024]{0:T(1024)S(1)} %bitcast.266, ...), kind=kOutput, calls=%fused_computation.60 | convolution fusion | flops 81887232 | bytes 483336 | tf_op jit(solution)/shard_map/dot_general | solution.py:115
  382.0 0.4 convolution_select_fusion.13
  382.4 0.4 fusion.103
  382.9 0.4 fusion.102
  383.3 0.4 fusion.101
  383.7 0.4 fusion.100
  384.1 0.4 fusion.99
  384.5 1.0 fusion.98
  385.5 1.9 fusion.107
  387.4 1.4 constant_dynamic-slice_fusion.13
  388.8 0.7 fusion.348
  393.8 1.3 collective-permute-start
  395.1 1.1 convolution_select_fusion
  396.2 2.0 collective-permute-start.9
  398.3 1.1 convolution_select_fusion.1
  399.4 1.9 collective-permute-start.8
  401.3 1.1 convolution_select_fusion.2
  402.4 3.4 collective-permute-start.7
  405.8 1.1 convolution_select_fusion.3
  406.9 3.8 collective-permute-start.6
  410.7 1.1 convolution_select_fusion.4
  411.8 0.4 fusion.108
  412.3 3.9 fusion.60
  416.2 4.0 fusion.45
  420.2 3.9 fusion.73
  424.2 4.1 fusion.53
  428.2 4.0 fusion.63
  432.3 3.9 fusion.67
  436.2 4.0 fusion.58
  440.2 4.8 %fusion.71 = f32[1,32,1024]{2,1,0:T(8,128)} fusion(f32[32,1024]{1,0:T(8,128)S(1)} %copy-done.40, f32[32,1024]{1,0:T(8,128)S(1)} %fusion.53, f32[1024]{0:T(1024)S(1)} %bitcast.319, f32[1024]{0:T(1024)S(1)} %bitcast.320, f32[1024]{0:T(1024)S(1)} %bitcast.318, f32[1024]{0:T(1024)S(1)} %bitcast.241, f32[1024]{0:T(1024)S(1)} %bitcast.248, ...), kind=kOutput, calls=%fused_computation.91 | convolution fusion | flops 81887232 | bytes 483336 | tf_op jit(solution)/shard_map/dot_general | solution.py:110
  445.0 1.8 fusion.37
  446.8 1.5 fusion.86
  448.3 1.5 fusion.87
  449.9 0.9 fusion.88
  450.7 0.9 fusion.89
  451.6 0.7 pad_maximum_fusion.1
  (114 shorter events, 0.7 us)
Async XLA Ops:
  0.0 5.8 %copy-start = (bf16[4,1024,256]{2,1,0:T(8,128)(2,1)S(1)}, bf16[4,1024,256]{2,1,0:T(8,128)(2,1)}, u32[]{:S(2)}) copy-start(bf16[4,1024,256]{2,1,0:T(8,128)(2,1)} %param.15) | copy-start | bytes 6291460
  0.0 4.2 copy-start.36
  0.9 3.3 copy-start.10
  1.0 3.3 copy-start.11
  1.0 3.3 copy-start.8
  1.0 4.8 %copy-start.6 = (s32[1,1024]{1,0:T(1,128)}, s32[1,1024]{1,0:T(1,128)S(1)}, u32[]{:S(2)}) copy-start(s32[1,1024]{1,0:T(1,128)S(1)} %get-tuple-element.79) | copy-start | bytes 12292
  5.0 1.3 copy-start.1
  5.0 21.1 %copy-start.2 = (f32[4,3,1024]{2,0,1:T(4,128)S(1)}, f32[4,3,1024]{2,0,1:T(4,128)}, u32[]{:S(2)}) copy-start(f32[4,3,1024]{2,0,1:T(4,128)} %param.13) | copy-start | bytes 147460
  5.8 20.4 %copy-start.12 = (s32[4,5]{1,0:T(4,128)S(1)}, s32[4,5]{1,0:T(4,128)}, u32[]{:S(2)}) copy-start(s32[4,5]{1,0:T(4,128)} %param.20) | copy-start | bytes 244
  5.8 21.7 %copy-start.4 = (f32[8,3,256]{2,0,1:T(8,128)S(1)}, f32[8,3,256]{2,0,1:T(8,128)}, u32[]{:S(2)}) copy-start(f32[8,3,256]{2,0,1:T(8,128)} %param.19) | copy-start | bytes 73732
  5.8 23.6 %copy-start.3 = (bf16[1,256,256]{2,1,0:T(8,128)(2,1)S(1)}, bf16[1,256,256]{2,1,0:T(8,128)(2,1)}, u32[]{:S(2)}) copy-start(bf16[1,256,256]{2,1,0:T(8,128)(2,1)} %param.17) | copy-start | bytes 393220
  6.5 387.3 %collective-permute-start.5 = (bf16[32,256]{1,0:T(8,128)(2,1)S(1)}, bf16[32,256]{1,0:T(8,128)(2,1)}, u32[]{:S(2)}, u32[]{:S(2)}) collective-permute-start(bf16[32,256]{1,0:T(8,128)(2,1)S(1)} %convolution_convert_fusion.2), channel_id=1, source_target_pairs={{4,0},{5,1},{6,2},{7,3},{8,4},{9,5},{10,6},{11,7},{12,8},{13,9},{1... | collective-permute-start | bytes 49160 | tf_op jit(solution)/shard_map/ppermute | solution.py:30
  7.8 388.4 %collective-permute-start.4 = (bf16[32,256]{1,0:T(8,128)(2,1)S(1)}, bf16[32,256]{1,0:T(8,128)(2,1)}, u32[]{:S(2)}, u32[]{:S(2)}) collective-permute-start(bf16[32,256]{1,0:T(8,128)(2,1)S(1)} %convolution_convert_fusion.2), channel_id=1, source_target_pairs={{3,0},{4,1},{5,2},{6,3},{7,4},{8,5},{9,6},{10,7},{11,8},{12,9},{13... | collective-permute-start | bytes 49160 | tf_op jit(solution)/shard_map/ppermute | solution.py:30
  9.1 390.2 %collective-permute-start.3 = (bf16[32,256]{1,0:T(8,128)(2,1)S(1)}, bf16[32,256]{1,0:T(8,128)(2,1)}, u32[]{:S(2)}, u32[]{:S(2)}) collective-permute-start(bf16[32,256]{1,0:T(8,128)(2,1)S(1)} %convolution_convert_fusion.2), channel_id=1, source_target_pairs={{2,0},{3,1},{4,2},{5,3},{6,4},{7,5},{8,6},{9,7},{10,8},{11,9},{12,... | collective-permute-start | bytes 49160 | tf_op jit(solution)/shard_map/ppermute | solution.py:30
  10.4 392.0 %collective-permute-start.2 = (bf16[32,256]{1,0:T(8,128)(2,1)S(1)}, bf16[32,256]{1,0:T(8,128)(2,1)}, u32[]{:S(2)}, u32[]{:S(2)}) collective-permute-start(bf16[32,256]{1,0:T(8,128)(2,1)S(1)} %convolution_convert_fusion.2), channel_id=1, source_target_pairs={{0,2},{1,3},{2,4},{3,5},{4,6},{5,7},{6,8},{7,9},{8,10},{9,11},{10,... | collective-permute-start | bytes 49160 | tf_op jit(solution)/shard_map/ppermute | solution.py:30
  17.4 389.5 %collective-permute-start.1 = (bf16[32,256]{1,0:T(8,128)(2,1)S(1)}, bf16[32,256]{1,0:T(8,128)(2,1)}, u32[]{:S(2)}, u32[]{:S(2)}) collective-permute-start(bf16[32,256]{1,0:T(8,128)(2,1)S(1)} %convolution_convert_fusion.2), channel_id=1, source_target_pairs={{0,3},{1,4},{2,5},{3,6},{4,7},{5,8},{6,9},{7,10},{8,11},{9,12},{10... | collective-permute-start | bytes 49160 | tf_op jit(solution)/shard_map/ppermute | solution.py:30
  358.4 5.5 %copy-start.45 = (f32[32,1024]{1,0:T(8,128)S(1)}, f32[32,1024]{1,0:T(8,128)}, u32[]{:S(2)}) copy-start(f32[32,1024]{1,0:T(8,128)} %fusion.75) | copy-start | bytes 393220
  363.9 4.0 copy-start.44
  372.1 4.9 %copy-start.39 = (f32[32,1024]{1,0:T(8,128)S(1)}, f32[32,1024]{1,0:T(8,128)}, u32[]{:S(2)}) copy-start(f32[32,1024]{1,0:T(8,128)} %fusion.51) | copy-start | bytes 393220
  377.0 5.0 %copy-start.13 = (f32[1,1,256]{2,0,1:T(1,128)S(1)}, f32[1,1,256]{2,0,1:T(1,128)}, u32[]{:S(2)}) copy-start(f32[1,1,256]{2,0,1:T(1,128)} %get-tuple-element.53) | copy-start | bytes 3076
  377.0 5.0 %copy-start.14 = (f32[1,1,256]{2,0,1:T(1,128)S(1)}, f32[1,1,256]{2,0,1:T(1,128)}, u32[]{:S(2)}) copy-start(f32[1,1,256]{2,0,1:T(1,128)} %get-tuple-element.54) | copy-start | bytes 3076
  377.0 5.0 %copy-start.33 = (f32[1,1,256]{2,0,1:T(1,128)S(1)}, f32[1,1,256]{2,0,1:T(1,128)}, u32[]{:S(2)}) copy-start(f32[1,1,256]{2,0,1:T(1,128)} %get-tuple-element.74) | copy-start | bytes 3076
  377.0 5.0 %copy-start.34 = (f32[1,1,256]{2,0,1:T(1,128)S(1)}, f32[1,1,256]{2,0,1:T(1,128)}, u32[]{:S(2)}) copy-start(f32[1,1,256]{2,0,1:T(1,128)} %get-tuple-element.75) | copy-start | bytes 3076
  377.0 5.0 %copy-start.35 = (f32[1,1,256]{2,0,1:T(1,128)S(1)}, f32[1,1,256]{2,0,1:T(1,128)}, u32[]{:S(2)}) copy-start(f32[1,1,256]{2,0,1:T(1,128)} %get-tuple-element.77) | copy-start | bytes 3076
  377.0 5.4 %copy-start.27 = (f32[1,1,256]{2,0,1:T(1,128)S(1)}, f32[1,1,256]{2,0,1:T(1,128)}, u32[]{:S(2)}) copy-start(f32[1,1,256]{2,0,1:T(1,128)} %get-tuple-element.71) | copy-start | bytes 3076
  377.0 5.4 %copy-start.28 = (f32[1,1,256]{2,0,1:T(1,128)S(1)}, f32[1,1,256]{2,0,1:T(1,128)}, u32[]{:S(2)}) copy-start(f32[1,1,256]{2,0,1:T(1,128)} %get-tuple-element.72) | copy-start | bytes 3076
  377.0 5.4 %copy-start.29 = (f32[1,1,256]{2,0,1:T(1,128)S(1)}, f32[1,1,256]{2,0,1:T(1,128)}, u32[]{:S(2)}) copy-start(f32[1,1,256]{2,0,1:T(1,128)} %get-tuple-element.73) | copy-start | bytes 3076
  377.0 5.8 %copy-start.30 = (f32[1,1,256]{2,0,1:T(1,128)S(1)}, f32[1,1,256]{2,0,1:T(1,128)}, u32[]{:S(2)}) copy-start(f32[1,1,256]{2,0,1:T(1,128)} %get-tuple-element.67) | copy-start | bytes 3076
  377.0 5.8 %copy-start.31 = (f32[1,1,256]{2,0,1:T(1,128)S(1)}, f32[1,1,256]{2,0,1:T(1,128)}, u32[]{:S(2)}) copy-start(f32[1,1,256]{2,0,1:T(1,128)} %get-tuple-element.68) | copy-start | bytes 3076
  377.0 5.8 %copy-start.32 = (f32[1,1,256]{2,0,1:T(1,128)S(1)}, f32[1,1,256]{2,0,1:T(1,128)}, u32[]{:S(2)}) copy-start(f32[1,1,256]{2,0,1:T(1,128)} %get-tuple-element.69) | copy-start | bytes 3076
  381.9 1.3 copy-start.24
  381.9 1.3 copy-start.25
  381.9 1.3 copy-start.26
  381.9 1.7 copy-start.21
  382.0 1.7 copy-start.22
  382.0 1.7 copy-start.23
  382.4 1.7 copy-start.18
  382.4 1.7 copy-start.19
  382.4 1.7 copy-start.20
  382.8 1.6 copy-start.15
  382.8 1.6 copy-start.16
  382.8 1.7 copy-start.17
  383.7 5.1 %copy-start.5 = (s32[1,9]{1,0:T(1,128)S(1)}, s32[1,9]{1,0:T(1,128)}, u32[]{:S(2)}) copy-start(s32[1,9]{1,0:T(1,128)} %param.21) | copy-start | bytes 112
  393.8 18.0 %collective-permute-start = (bf16[32,256]{1,0:T(8,128)(2,1)S(1)}, bf16[32,256]{1,0:T(8,128)(2,1)S(1)}, u32[]{:S(2)}, u32[]{:S(2)}) collective-permute-start(bf16[32,256]{1,0:T(8,128)(2,1)S(1)} %convolution_convert_fusion.2), channel_id=1, source_target_pairs={{0,4},{1,5},{2,6},{3,7},{4,8},{5,9},{6,10},{7,11},{8,12},{9,13},{1... | collective-permute-start | bytes 49160 | tf_op jit(solution)/shard_map/ppermute | solution.py:30
  396.2 15.6 %copy-start.37 = (f32[32,256]{1,0:T(8,128)S(1)}, f32[32,256]{1,0:T(8,128)}, u32[]{:S(2)}) copy-start(f32[32,256]{1,0:T(8,128)} %fusion.107) | copy-start | bytes 98308
  396.2 16.0 %collective-permute-start.9 = (f32[2,3,1024]{2,0,1:T(2,128)S(1)}, f32[2,3,1024]{2,0,1:T(2,128)S(1)}, u32[]{:S(2)}, u32[]{:S(2)}) collective-permute-start(f32[2,3,1024]{2,0,1:T(2,128)S(1)} %get-tuple-element.27), channel_id=1, source_target_pairs={{1,0},{2,1},{3,2},{4,3},{5,4},{6,5},{7,6},{8,7},{9,8},{10,9},{11,1... | collective-permute-start | bytes 73736 | tf_op jit(solution)/shard_map/ppermute | solution.py:23
  399.4 12.9 %collective-permute-start.8 = (bf16[2,32,1024]{2,1,0:T(8,128)(2,1)S(1)}, bf16[2,32,1024]{2,1,0:T(8,128)(2,1)S(1)}, u32[]{:S(2)}, u32[]{:S(2)}) collective-permute-start(bf16[2,32,1024]{2,1,0:T(8,128)(2,1)S(1)} %pad_maximum_fusion.3), channel_id=1, source_target_pairs={{1,0},{2,1},{3,2},{4,3},{5,4},{6,5},{7,6},{8,7},{9,8},{10,9},{11,1... | collective-permute-start | bytes 393224 | tf_op jit(solution)/shard_map/ppermute | solution.py:23
  401.3 11.0 %copy-start.43 = (f32[32,1024]{1,0:T(8,128)S(1)}, f32[32,1024]{1,0:T(8,128)}, u32[]{:S(2)}) copy-start(f32[32,1024]{1,0:T(8,128)} %fusion.42) | copy-start | bytes 393220
  402.4 9.8 %collective-permute-start.7 = (f32[2,3,1024]{2,0,1:T(2,128)S(1)}, f32[2,3,1024]{2,0,1:T(2,128)S(1)}, u32[]{:S(2)}, u32[]{:S(2)}) collective-permute-start(f32[2,3,1024]{2,0,1:T(2,128)S(1)} %get-tuple-element.26), channel_id=1, source_target_pairs={{0,1},{1,2},{2,3},{3,4},{4,5},{5,6},{6,7},{7,8},{8,9},{9,10},{10,1... | collective-permute-start | bytes 73736 | tf_op jit(solution)/shard_map/ppermute | solution.py:22
  406.9 13.3 %collective-permute-start.6 = (bf16[2,32,1024]{2,1,0:T(8,128)(2,1)S(1)}, bf16[2,32,1024]{2,1,0:T(8,128)(2,1)S(1)}, u32[]{:S(2)}, u32[]{:S(2)}) collective-permute-start(bf16[2,32,1024]{2,1,0:T(8,128)(2,1)S(1)} %pad_maximum_fusion.2), channel_id=1, source_target_pairs={{0,1},{1,2},{2,3},{3,4},{4,5},{5,6},{6,7},{7,8},{8,9},{9,10},{10,1... | collective-permute-start | bytes 393224 | tf_op jit(solution)/shard_map/ppermute | solution.py:22
  416.2 4.0 copy-start.46
  424.1 4.1 copy-start.38
  428.2 4.0 copy-start.41
  428.2 4.0 copy-start.42
  436.1 4.0 copy-start.40
  446.8 3.1 copy-start.9
  446.8 4.0 copy-start.7

commit v2 on v1

--- a/solution.py
+++ b/solution.py
@@ -1,13 +1,15 @@
 import jax
 import jax.numpy as jnp
 from jax import lax
+from jax.experimental import pallas as pl
+from jax.experimental.pallas import tpu as pltpu
 from jax.sharding import Mesh
 from jax.sharding import PartitionSpec as P
 
 NEAR_REACH = 2
 COUPLE_REACH = 4
-GROUP_DEV = ("group", "dev_0", "dev_1")
-DEV = ("dev_0", "dev_1")
+GROUP_DEV = ("group", "dev_0", "dev_1", "dev_2")
+DEV = ("dev_0", "dev_1", "dev_2")
 
 
 ROOT_THREE = 1.7320508075688772
@@ -30,12 +32,75 @@
     return lax.ppermute(block, axis, route)
 
 
+def from_everyone(value, axis):
+    peers = lax.axis_size(axis)
+    return lax.all_to_all(
+        jnp.broadcast_to(value[None], (peers, *value.shape)), axis, 0, 0, tiled=True
+    )
+
+
 def matern(source, target, amplitude):
     square = (source[0][:, None] - target[0][None, :]) ** 2
     square = square + (source[1][:, None] - target[1][None, :]) ** 2
     square = square + (source[2][:, None] - target[2][None, :]) ** 2
     scaled = jnp.sqrt(square) * (ROOT_THREE / LENGTH_SCALE)
     return (amplitude * (1.0 + scaled) * jnp.exp(-scaled)).astype(jnp.bfloat16)
+
+
+def near_kernel(pattern_ref, amp_ref, target_ref, source_ref, probes_ref, out_ref, tile_ref):
+    t = pl.program_id(0)
+    window = 2 * NEAR_REACH + 1
+    size = target_ref.shape[-1]
+    chunk = tile_ref.shape[0]
+    rows = 16
+    amp = amp_ref[0]
+    tx = target_ref[0, 0:1, :]
+    ty = target_ref[0, 1:2, :]
+    tz = target_ref[0, 2:3, :]
+    out_ref[0] = jnp.zeros(out_ref.shape[1:], jnp.float32)
+    for o in range(window):
+        s = t + o
+
+        @pl.when(pattern_ref[t, o] != 0)
+        def _():
+            def body(c, carry):
+                start = pl.multiple_of(c * chunk, chunk)
+                for r in range(chunk // rows):
+                    col = source_ref[s, pl.ds(start + r * rows, rows), :]
+                    dx = col[:, 0:1] - tx
+                    dy = col[:, 1:2] - ty
+                    dz = col[:, 2:3] - tz
+                    square = dx * dx
+                    square = square + dy * dy
+                    square = square + dz * dz
+                    scaled = jnp.sqrt(square) * (ROOT_THREE / LENGTH_SCALE)
+                    value = amp * (1.0 + scaled) * jnp.exp(-scaled)
+                    tile_ref[r * rows : (r + 1) * rows, :] = value.astype(jnp.bfloat16)
+                values = probes_ref[s, :, pl.ds(start, chunk)]
+                out_ref[0] += jnp.dot(values, tile_ref[...], preferred_element_type=jnp.float32)
+                return carry
+
+            lax.fori_loop(0, size // chunk, body, 0)
+
+
+def near_field(pattern, amplitude, targets, sources_t, wide_probes):
+    leaves, _, size = targets.shape
+    probe_count = wide_probes.shape[1]
+    chunk = 128
+    return pl.pallas_call(
+        near_kernel,
+        grid=(leaves,),
+        in_specs=[
+            pl.BlockSpec(memory_space=pltpu.SMEM),
+            pl.BlockSpec(memory_space=pltpu.SMEM),
+            pl.BlockSpec((1, 3, size), lambda t: (t, 0, 0)),
+            pl.BlockSpec(sources_t.shape, lambda t: (0, 0, 0)),
+            pl.BlockSpec(wide_probes.shape, lambda t: (0, 0, 0)),
+        ],
+        out_specs=pl.BlockSpec((1, probe_count, size), lambda t: (t, 0, 0)),
+        out_shape=jax.ShapeDtypeStruct((leaves, probe_count, size), jnp.float32),
+        scratch_shapes=[pltpu.VMEM((chunk, size), jnp.bfloat16)],
+    )(pattern, amplitude.reshape(1), targets, sources_t, wide_probes)
 
 
 def one_hot(ordering, size):
@@ -76,9 +141,6 @@
     transfer_flat = node_transfer[0].reshape(leaf_count * skeleton, skeleton)
     node_coef = jnp.dot(stacked, transfer_flat, preferred_element_type=f32).astype(jnp.bfloat16)
     group_term = jnp.dot(node_coef, group_transfer[0], preferred_element_type=f32)
-    own_coef = lax.psum(group_term, DEV).astype(jnp.bfloat16)
-    group_coef = lax.all_gather(own_coef, "group", axis=0, tiled=False)
-
     node_index = lax.axis_index(DEV)
     node_total = lax.axis_size(DEV)
     relayed = {}
@@ -89,36 +151,36 @@
 
     wide_probes = with_halo(ordered, GROUP_DEV, NEAR_REACH)
     wide_points = with_halo(points, GROUP_DEV, NEAR_REACH)
-    wide = leaf_count + 2 * NEAR_REACH
-    own = range(NEAR_REACH, NEAR_REACH + leaf_count)
-    pattern = near_pattern.astype(f32)
-    near = [jnp.zeros((probe_count, leaf_size), f32) for _ in range(leaf_count)]
-    for b in own:
-        tile = matern(wide_points[b], wide_points[b], signal_variance)
-        t = b - NEAR_REACH
-        near[t] = near[t] + jnp.dot(
-            wide_probes[b], tile, preferred_element_type=f32
-        ) * pattern[t, NEAR_REACH]
-    for gap in range(1, NEAR_REACH + 1):
-        for a in range(wide - gap):
-            b = a + gap
-            if a not in own and b not in own:
-                continue
-            tile = matern(wide_points[a], wide_points[b], signal_variance)
-            if b in own:
-                t = b - NEAR_REACH
-                near[t] = near[t] + jnp.dot(
-                    wide_probes[a], tile, preferred_element_type=f32
-                ) * pattern[t, NEAR_REACH - gap]
-            if a in own:
-                t = a - NEAR_REACH
-                near[t] = near[t] + lax.dot_general(
-                    wide_probes[b], tile, (((1,), (1,)), ((), ())), preferred_element_type=f32
-                ) * pattern[t, NEAR_REACH + gap]
-    near = jnp.stack(near)
-
+    sources_t = jnp.transpose(wide_points, (0, 2, 1))
+    window = 2 * NEAR_REACH + 1
+
+    rounds = ["dev_0", "dev_2", "dev_1"]
+    running = group_term
     group_index = lax.axis_index("group")
     group_total = lax.axis_size("group")
+    parts = []
+    for step in range(leaf_count):
+        running, points_of, probes_of, sources_of = lax.optimization_barrier(
+            (running, wide_points, wide_probes, sources_t)
+        )
+        if step < len(rounds):
+            received = from_everyone(running, rounds[step])
+        else:
+            own_coef = running.astype(jnp.bfloat16)
+            group_coef = from_everyone(own_coef, "group")
+        parts.append(
+            near_field(
+                near_pattern[step : step + 1],
+                signal_variance,
+                points_of[step + NEAR_REACH : step + NEAR_REACH + 1],
+                sources_of[step : step + window],
+                probes_of[step : step + window],
+            )
+        )
+        if step < len(rounds):
+            running = jnp.sum(received, axis=0)
+    near = jnp.concatenate(parts, axis=0)
+
     own_skeleton = lax.dynamic_index_in_dim(group_skeleton, group_index, 0, keepdims=False)
     far_group = jnp.zeros((probe_count, skeleton), f32)
     for other in range(group_total):
@@ -166,7 +228,7 @@
 
 
 def solution(mesh):
-    finer = Mesh(mesh.devices.reshape(mesh.shape["group"], 4, 16), ("group", "dev_0", "dev_1"))
+    finer = Mesh(mesh.devices.reshape(mesh.shape["group"], 4, 4, 4), GROUP_DEV)
     return jax.shard_map(
         on_device,
         mesh=finer,

time: 460 us -> 274 us (0.60); the launches traced: 453 us -> 272 us
  blocking collectives: 296 us -> 0 us
  Pallas kernels: 0 us -> 105 us
  matrix products: 112 us -> 35.9 us
  starting transfers between devices: 31.9 us -> 75.6 us
  local copies, waits for them, and re-layouts: 5.95 us -> 34 us
  waiting for transfers between devices: 0.03 us -> 12 us
    psum x1 -> x0, blocking collectives: 227 us -> none  [on_device(): own_coef = lax.psum(group_term, DEV).astype(jnp.bfloat16)]
    pallas_call x0 -> x4, Pallas kernels: none -> 105 us  [near_field(): pl.pallas_call(near_kernel, grid=(leaves,), in_specs=[pl.BlockSpec(memory...]
    dot_general x20 -> x0, matrix products: 89.1 us -> none  [the longest x8 36 us: on_device(): lax.dot_general(wide_probes[b], tile, (((1,), (1,)), ((), ())), preferred...]
    all_gather x1 -> x0, blocking collectives: 69.1 us -> none  [on_device(): group_coef = lax.all_gather(own_coef, 'group', axis=0, tiled=False)]
    all_to_all x0 -> x4, starting transfers between devices: none -> 28.1 us  [from_everyone(): lax.all_to_all(jnp.broadcast_to(value[None], (peers, *value.shape)), axis...]
    slice x2 -> x13, local copies, waits for them, and re-layouts: 1.3 us -> 20.5 us  [the longest x4 13.7 us: on_device(): sources_of[step:step + window]]
    ppermute x2, starting transfers between devices: 3.96 us -> 22.9 us  [with_halo(): high = lax.ppermute(leading, axis, [(b, a) for a, b in up])]
    all_to_all x0 -> x4, waiting for transfers between devices: none -> 10 us  [from_everyone(): lax.all_to_all(jnp.broadcast_to(value[None], (peers, *value.shape)), axis...]
  transfers between devices with their start and end apart: 10 -> 14, of which waited for: 0 -> 2; matrix products, arithmetic and copies ran while one was open for 18% -> 21% of each run, Pallas kernels for 0% -> 39%
where the time goes in v2:
time: 274 us; the launch traced here: 272 us
  Pallas kernels  105 us (38%)
  starting transfers between devices  75.6 us (28%)
  matrix products  35.9 us (13%)
  local copies, waits for them, and re-layouts  34 us (12%)
  waiting for transfers between devices  12 us (4%)
  between operations  5.19 us (2%)
  other arithmetic  4.37 us (2%)
    pallas_call x4, Pallas kernels, near_field(): pl.pallas_call(near_kernel, grid=(leaves,), in_specs=[pl.BlockSpec(memory...  105 us
    all_to_all x4, starting transfers between devices, from_everyone(): lax.all_to_all(jnp.broadcast_to(value[None], (peers, *value.shape)), axis...  28.1 us
    ppermute x2, starting transfers between devices, with_halo(): high = lax.ppermute(leading, axis, [(b, a) for a, b in up])  22.9 us
    ppermute x6, starting transfers between devices, from_behind(): return lax.ppermute(block, axis, route)  18.3 us
    slice x4, local copies, waits for them, and re-layouts, on_device(): sources_of[step:step + window]  13.7 us
    all_to_all x4, waiting for transfers between devices, from_everyone(): lax.all_to_all(jnp.broadcast_to(value[None], (peers, *value.shape)), axis...  10 us
    dot_general x6, matrix products, on_device(): jnp.dot(relayed[offset], kernel_tile, preferred_element_type=f32)  9.91 us
    dot_general x7, matrix products, on_device(): jnp.dot(group_coef[other], kernel_tile, preferred_element_type=f32)  8.57 us
  transfers between devices with their start and end apart: 14, of which 2 were waited for; matrix products, arithmetic and copies ran while one was open for 21% of the time, Pallas kernels for 39%

profile of v2, /device:TPU:1, one launch (start us, length us, event | category | flops | bytes accessed | tf_op | source)
XLA Modules:
  0.0 271.8 jit_solution(4409679455921692814)
XLA Ops:
  0.0 0.9 fusion.238
  1.0 1.6 fusion.27
  2.6 1.6 fusion.29
  4.2 4.4 %collective-permute-start.2 = (bf16[2,32,1024]{2,1,0:T(8,128)(2,1)S(1)}, bf16[2,32,1024]{2,1,0:T(8,128)(2,1)S(1)}, u32[]{:S(2)}, u32[]{:S(2)}) collective-permute-start(bf16[2,32,1024]{2,1,0:T(8,128)(2,1)S(1)} %pad_maximum_fusion.2), channel_id=1, source_target_pairs={{0,1},{1,2},{2,3},{3,4},{4,5},{5,6},{6,7},{7,8},{8,9},{9,10},{10,1... | collective-permute-start | bytes 393224 | tf_op jit(solution)/shard_map/ppermute | solution.py:24
  8.6 0.9 fusion.235
  9.5 12.5 %collective-permute-start.1 = (f32[2,3,1024]{2,0,1:T(2,128)S(1)}, f32[2,3,1024]{2,0,1:T(2,128)S(1)}, u32[]{:S(2)}, u32[]{:S(2)}) collective-permute-start(f32[2,3,1024]{2,0,1:T(2,128)S(1)} %get-tuple-element.59), channel_id=1, source_target_pairs={{1,0},{2,1},{3,2},{4,3},{5,4},{6,5},{7,6},{8,7},{9,8},{10,9},{11,1... | collective-permute-start | bytes 73736 | tf_op jit(solution)/shard_map/ppermute | solution.py:25
  22.0 1.9 collective-permute-start
  24.0 1.5 fusion.237
  25.5 1.7 fusion.236
  27.2 1.4 fusion.239
  28.7 2.1 constant_dynamic-slice_fusion.13
  30.8 0.8 pad_maximum_fusion.4
  31.6 2.7 copy.35
  34.3 1.6 constant_dynamic-update-slice_fusion.4
  36.0 1.6 constant_dynamic-update-slice_fusion.3
  38.3 1.3 collective-permute-start.9
  39.8 10.4 %collective-permute-start.3 = (bf16[2,32,1024]{2,1,0:T(8,128)(2,1)S(1)}, bf16[2,32,1024]{2,1,0:T(8,128)(2,1)S(1)}, u32[]{:S(2)}, u32[]{:S(2)}) collective-permute-start(bf16[2,32,1024]{2,1,0:T(8,128)(2,1)S(1)} %pad_maximum_fusion.3), channel_id=1, source_target_pairs={{1,0},{2,1},{3,2},{4,3},{5,4},{6,5},{7,6},{8,7},{9,8},{10,9},{11,1... | collective-permute-start | bytes 393224 | tf_op jit(solution)/shard_map/ppermute | solution.py:25
  50.2 1.9 collective-permute-done.3
  52.8 3.9 %all-to-all-start = ((f32[4,32,256]{2,1,0:T(8,128)}), f32[4,32,256]{2,1,0:T(8,128)}, u32[]{:S(2)}, u32[]{:S(2)}) async-start(f32[4,32,256]{2,1,0:T(8,128)} %broadcast_in_dim.41), calls=%async_computation | async-start | bytes 262144 | tf_op jit(solution)/shard_map/all_to_all | solution.py:37
  62.0 1.3 collective-permute-start.8
  63.3 1.3 collective-permute-start.7
  64.6 5.5 %collective-permute-start.6 = (bf16[32,256]{1,0:T(8,128)(2,1)S(1)}, bf16[32,256]{1,0:T(8,128)(2,1)}, u32[]{:S(2)}, u32[]{:S(2)}) collective-permute-start(bf16[32,256]{1,0:T(8,128)(2,1)S(1)} %convolution_convert_fusion.2), channel_id=1, source_target_pairs={{0,2},{1,3},{2,4},{3,5},{4,6},{5,7},{6,8},{7,9},{8,10},{9,11},{10,... | collective-permute-start | bytes 49160 | tf_op jit(solution)/shard_map/ppermute | solution.py:32
  70.1 7.0 %collective-permute-start.5 = (bf16[32,256]{1,0:T(8,128)(2,1)S(1)}, bf16[32,256]{1,0:T(8,128)(2,1)}, u32[]{:S(2)}, u32[]{:S(2)}) collective-permute-start(bf16[32,256]{1,0:T(8,128)(2,1)S(1)} %convolution_convert_fusion.2), channel_id=1, source_target_pairs={{0,3},{1,4},{2,5},{3,6},{4,7},{5,8},{6,9},{7,10},{8,11},{9,12},{10... | collective-permute-start | bytes 49160 | tf_op jit(solution)/shard_map/ppermute | solution.py:32
  77.1 0.9 reduce_sum.27
  78.0 0.7 broadcast_in_dim.42
  78.7 3.9 %all-to-all-start.1 = ((f32[4,32,256]{2,1,0:T(8,128)}), f32[4,32,256]{2,1,0:T(8,128)}, u32[]{:S(2)}, u32[]{:S(2)}) async-start(f32[4,32,256]{2,1,0:T(8,128)} %broadcast_in_dim.42), calls=%async_computation.1 | async-start | bytes 262144 | tf_op jit(solution)/shard_map/all_to_all | solution.py:37
  82.7 1.9 collective-permute-start.4
  84.6 1.7 convolution_select_fusion
  86.3 1.7 convolution_select_fusion.1
  88.0 0.9 reduce_sum.28
  89.6 12.2 %all-to-all-start.2 = ((f32[4,32,256]{2,1,0:T(8,128)}), f32[4,32,256]{2,1,0:T(8,128)}, u32[]{:S(2)}, u32[]{:S(2)}) async-start(f32[4,32,256]{2,1,0:T(8,128)} %broadcast_in_dim.43), calls=%async_computation.2 | async-start | bytes 262144 | tf_op jit(solution)/shard_map/all_to_all | solution.py:37
  101.8 1.7 convolution_select_fusion.2
  103.5 1.7 convolution_select_fusion.3
  105.3 10.0 %all-to-all-done.2 = f32[4,32,256]{2,1,0:T(8,128)} async-done(((f32[4,32,256]{2,1,0:T(8,128)}), f32[4,32,256]{2,1,0:T(8,128)}, u32[]{:S(2)}, u32[]{:S(2)}) %all-to-all-start.2) | async-done | bytes 131104 | tf_op jit(solution)/shard_map/all_to_all | solution.py:37
  115.3 0.9 reduce_sum.29
  116.9 8.1 %all-to-all-start.3 = ((bf16[8,32,256]{2,1,0:T(8,128)(2,1)}), bf16[8,32,256]{2,1,0:T(8,128)(2,1)}, u32[]{:S(2)}, u32[]{:S(2)}) async-start(bf16[8,32,256]{2,1,0:T(8,128)(2,1)} %broadcast_in_dim.44), calls=%async_computation.3 | async-start | bytes 262144 | tf_op jit(solution)/shard_map/all_to_all | solution.py:37
  125.0 1.7 convolution_select_fusion.4
  127.3 3.4 %slice.470.source_ref = f32[5,1024,3]{2,1,0:T(8,128)} slice(f32[8,1024,3]{2,1,0:T(8,128)} %bitcast.173), slice={[0:5], [0:1024], [0:3]} | slice | bytes 122880 | tf_op jit(solution)/shard_map/slice | solution.py:176
  130.8 0.7 slice.471.probes_ref
  131.5 26.1 %shard_map.118 = f32[1,32,1024]{2,1,0:T(8,128)} custom-call(s32[1,5]{1,0:T(1,128)} %get-tuple-element.91.pattern_ref, f32[1]{0:T(128)} %bitcast.169.amp_ref, f32[1,3,1024]{2,1,0:T(4,128)} %slice.496.target_ref, f32[5,1024,3]{2,1,0:T(8,128)} %slice.470.source_ref, bf16[5,32,1024]{2,1,0:T(8,128)(2,1)} %slice.471.probes_ref), custom_call_target="tpu_custom_call" | custom-call | tf_op jit(solution)/shard_map/pallas_call | solution.py:90
  158.3 3.4 %slice.474.source_ref = f32[5,1024,3]{2,1,0:T(8,128)} slice(f32[8,1024,3]{2,1,0:T(8,128)} %bitcast.174), slice={[1:6], [0:1024], [0:3]} | slice | bytes 122880 | tf_op jit(solution)/shard_map/slice | solution.py:176
  161.7 0.7 slice.475.probes_ref
  162.4 26.3 %shard_map.119 = f32[1,32,1024]{2,1,0:T(8,128)} custom-call(s32[1,5]{1,0:T(1,128)} %get-tuple-element.92.pattern_ref, f32[1]{0:T(128)} %bitcast.170.amp_ref, f32[1,3,1024]{2,1,0:T(4,128)} %slice.497.target_ref, f32[5,1024,3]{2,1,0:T(8,128)} %slice.474.source_ref, bf16[5,32,1024]{2,1,0:T(8,128)(2,1)} %slice.475.probes_ref), custom_call_target="tpu_custom_call" | custom-call | tf_op jit(solution)/shard_map/pallas_call | solution.py:90
  189.4 3.4 %slice.478.source_ref = f32[5,1024,3]{2,1,0:T(8,128)} slice(f32[8,1024,3]{2,1,0:T(8,128)} %bitcast.175), slice={[2:7], [0:1024], [0:3]} | slice | bytes 122880 | tf_op jit(solution)/shard_map/slice | solution.py:176
  192.8 0.7 slice.479.probes_ref
  193.5 26.1 %shard_map.120 = f32[1,32,1024]{2,1,0:T(8,128)} custom-call(s32[1,5]{1,0:T(1,128)} %get-tuple-element.94.pattern_ref, f32[1]{0:T(128)} %bitcast.171.amp_ref, f32[1,3,1024]{2,1,0:T(4,128)} %slice.498.target_ref, f32[5,1024,3]{2,1,0:T(8,128)} %slice.478.source_ref, bf16[5,32,1024]{2,1,0:T(8,128)(2,1)} %slice.479.probes_ref), custom_call_target="tpu_custom_call" | custom-call | tf_op jit(solution)/shard_map/pallas_call | solution.py:90
  220.3 3.4 %slice.482.source_ref = f32[5,1024,3]{2,1,0:T(8,128)} slice(f32[8,1024,3]{2,1,0:T(8,128)} %bitcast.176), slice={[3:8], [0:1024], [0:3]} | slice | bytes 122880 | tf_op jit(solution)/shard_map/slice | solution.py:176
  223.7 0.7 slice.483.probes_ref
  224.5 26.3 %shard_map.121 = f32[1,32,1024]{2,1,0:T(8,128)} custom-call(s32[1,5]{1,0:T(1,128)} %get-tuple-element.93.pattern_ref, f32[1]{0:T(128)} %bitcast.172.amp_ref, f32[1,3,1024]{2,1,0:T(4,128)} %slice.499.target_ref, f32[5,1024,3]{2,1,0:T(8,128)} %slice.482.source_ref, bf16[5,32,1024]{2,1,0:T(8,128)(2,1)} %slice.483.probes_ref), custom_call_target="tpu_custom_call" | custom-call | tf_op jit(solution)/shard_map/pallas_call | solution.py:90
  250.8 1.2 convolution_select_fusion.13
  251.9 1.2 fusion.47
  253.1 1.1 fusion.46
  254.2 1.1 fusion.45
  255.4 1.1 fusion.44
  256.5 1.1 fusion.43
  257.6 1.7 fusion.42
  259.4 1.9 fusion.51
  261.3 1.3 fusion.52
  262.6 1.6 fusion.17
  264.2 1.7 fusion.26
  265.9 1.7 fusion.28
  267.6 1.7 fusion.30
  269.3 1.7 fusion.32
  271.0 0.7 pad_maximum_fusion.1
  (68 shorter events, 6.3 us)
Async XLA Ops:
  0.0 37.6 %copy-start = (bf16[4,1024,256]{2,1,0:T(8,128)(2,1)S(1)}, bf16[4,1024,256]{2,1,0:T(8,128)(2,1)}, u32[]{:S(2)}) copy-start(bf16[4,1024,256]{2,1,0:T(8,128)(2,1)} %param.15) | copy-start | bytes 6291460
  0.9 1.6 copy-start.15
  0.9 23.0 %copy-start.13 = (s32[1,1024]{1,0:T(1,128)}, s32[1,1024]{1,0:T(1,128)S(1)}, u32[]{:S(2)}) copy-start(s32[1,1024]{1,0:T(1,128)S(1)} %get-tuple-element.90) | copy-start | bytes 12292
  1.0 35.0 %copy-start.9 = (s32[1,1024]{1,0:T(1,128)}, s32[1,1024]{1,0:T(1,128)S(1)}, u32[]{:S(2)}) copy-start(s32[1,1024]{1,0:T(1,128)S(1)} %get-tuple-element.87) | copy-start | bytes 12292
  1.0 35.0 %copy-start.11 = (s32[1,1024]{1,0:T(1,128)}, s32[1,1024]{1,0:T(1,128)S(1)}, u32[]{:S(2)}) copy-start(s32[1,1024]{1,0:T(1,128)S(1)} %get-tuple-element.88) | copy-start | bytes 12292
  4.2 30.1 %collective-permute-start.2 = (bf16[2,32,1024]{2,1,0:T(8,128)(2,1)S(1)}, bf16[2,32,1024]{2,1,0:T(8,128)(2,1)S(1)}, u32[]{:S(2)}, u32[]{:S(2)}) collective-permute-start(bf16[2,32,1024]{2,1,0:T(8,128)(2,1)S(1)} %pad_maximum_fusion.2), channel_id=1, source_target_pairs={{0,1},{1,2},{2,3},{3,4},{4,5},{5,6},{6,7},{7,8},{8,9},{9,10},{10,1... | collective-permute-start | bytes 393224 | tf_op jit(solution)/shard_map/ppermute | solution.py:24
  9.5 21.2 %collective-permute-start.1 = (f32[2,3,1024]{2,0,1:T(2,128)S(1)}, f32[2,3,1024]{2,0,1:T(2,128)S(1)}, u32[]{:S(2)}, u32[]{:S(2)}) collective-permute-start(f32[2,3,1024]{2,0,1:T(2,128)S(1)} %get-tuple-element.59), channel_id=1, source_target_pairs={{1,0},{2,1},{3,2},{4,3},{5,4},{6,5},{7,6},{8,7},{9,8},{10,9},{11,1... | collective-permute-start | bytes 73736 | tf_op jit(solution)/shard_map/ppermute | solution.py:25
  22.0 8.7 %collective-permute-start = (f32[2,3,1024]{2,0,1:T(2,128)S(1)}, f32[2,3,1024]{2,0,1:T(2,128)S(1)}, u32[]{:S(2)}, u32[]{:S(2)}) collective-permute-start(f32[2,3,1024]{2,0,1:T(2,128)S(1)} %get-tuple-element.58), channel_id=1, source_target_pairs={{0,1},{1,2},{2,3},{3,4},{4,5},{5,6},{6,7},{7,8},{8,9},{9,10},{10,1... | collective-permute-start | bytes 73736 | tf_op jit(solution)/shard_map/ppermute | solution.py:24
  31.6 6.5 %copy-start.1 = (bf16[1,4,256,256]{3,2,1,0:T(8,128)(2,1)S(1)}, bf16[1,4,256,256]{3,2,1,0:T(8,128)(2,1)}, u32[]{:S(2)}) copy-start(bf16[1,4,256,256]{3,2,1,0:T(8,128)(2,1)} %param.16) | copy-start | bytes 1572868
  34.3 5.3 %copy-start.6 = (bf16[1,256,256]{2,1,0:T(8,128)(2,1)S(1)}, bf16[1,256,256]{2,1,0:T(8,128)(2,1)}, u32[]{:S(2)}) copy-start(bf16[1,256,256]{2,1,0:T(8,128)(2,1)} %param.17) | copy-start | bytes 393220
  34.3 22.4 %copy-start.8 = (s32[1,9]{1,0:T(1,128)S(1)}, s32[1,9]{1,0:T(1,128)}, u32[]{:S(2)}) copy-start(s32[1,9]{1,0:T(1,128)} %param.21) | copy-start | bytes 112
  38.3 44.4 %collective-permute-start.9 = (bf16[32,256]{1,0:T(8,128)(2,1)S(1)}, bf16[32,256]{1,0:T(8,128)(2,1)}, u32[]{:S(2)}, u32[]{:S(2)}) collective-permute-start(bf16[32,256]{1,0:T(8,128)(2,1)S(1)} %convolution_convert_fusion.2), channel_id=1, source_target_pairs={{4,0},{5,1},{6,2},{7,3},{8,4},{9,5},{10,6},{11,7},{12,8},{13,9},{1... | collective-permute-start | bytes 49160 | tf_op jit(solution)/shard_map/ppermute | solution.py:32
  39.8 12.3 %collective-permute-start.3 = (bf16[2,32,1024]{2,1,0:T(8,128)(2,1)S(1)}, bf16[2,32,1024]{2,1,0:T(8,128)(2,1)S(1)}, u32[]{:S(2)}, u32[]{:S(2)}) collective-permute-start(bf16[2,32,1024]{2,1,0:T(8,128)(2,1)S(1)} %pad_maximum_fusion.3), channel_id=1, source_target_pairs={{1,0},{2,1},{3,2},{4,3},{5,4},{6,5},{7,6},{8,7},{9,8},{10,9},{11,1... | collective-permute-start | bytes 393224 | tf_op jit(solution)/shard_map/ppermute | solution.py:25
  52.8 24.4 %all-to-all-start = ((f32[4,32,256]{2,1,0:T(8,128)}), f32[4,32,256]{2,1,0:T(8,128)}, u32[]{:S(2)}, u32[]{:S(2)}) async-start(f32[4,32,256]{2,1,0:T(8,128)} %broadcast_in_dim.41), calls=%async_computation | async-start | bytes 262144 | tf_op jit(solution)/shard_map/all_to_all | solution.py:37
  62.0 24.3 %collective-permute-start.8 = (bf16[32,256]{1,0:T(8,128)(2,1)S(1)}, bf16[32,256]{1,0:T(8,128)(2,1)}, u32[]{:S(2)}, u32[]{:S(2)}) collective-permute-start(bf16[32,256]{1,0:T(8,128)(2,1)S(1)} %convolution_convert_fusion.2), channel_id=1, source_target_pairs={{3,0},{4,1},{5,2},{6,3},{7,4},{8,5},{9,6},{10,7},{11,8},{12,9},{13... | collective-permute-start | bytes 49160 | tf_op jit(solution)/shard_map/ppermute | solution.py:32
  63.3 38.5 %collective-permute-start.7 = (bf16[32,256]{1,0:T(8,128)(2,1)S(1)}, bf16[32,256]{1,0:T(8,128)(2,1)}, u32[]{:S(2)}, u32[]{:S(2)}) collective-permute-start(bf16[32,256]{1,0:T(8,128)(2,1)S(1)} %convolution_convert_fusion.2), channel_id=1, source_target_pairs={{2,0},{3,1},{4,2},{5,3},{6,4},{7,5},{8,6},{9,7},{10,8},{11,9},{12,... | collective-permute-start | bytes 49160 | tf_op jit(solution)/shard_map/ppermute | solution.py:32
  64.6 38.9 %collective-permute-start.6 = (bf16[32,256]{1,0:T(8,128)(2,1)S(1)}, bf16[32,256]{1,0:T(8,128)(2,1)}, u32[]{:S(2)}, u32[]{:S(2)}) collective-permute-start(bf16[32,256]{1,0:T(8,128)(2,1)S(1)} %convolution_convert_fusion.2), channel_id=1, source_target_pairs={{0,2},{1,3},{2,4},{3,5},{4,6},{5,7},{6,8},{7,9},{8,10},{9,11},{10,... | collective-permute-start | bytes 49160 | tf_op jit(solution)/shard_map/ppermute | solution.py:32
  70.1 54.8 %collective-permute-start.5 = (bf16[32,256]{1,0:T(8,128)(2,1)S(1)}, bf16[32,256]{1,0:T(8,128)(2,1)}, u32[]{:S(2)}, u32[]{:S(2)}) collective-permute-start(bf16[32,256]{1,0:T(8,128)(2,1)S(1)} %convolution_convert_fusion.2), channel_id=1, source_target_pairs={{0,3},{1,4},{2,5},{3,6},{4,7},{5,8},{6,9},{7,10},{8,11},{9,12},{10... | collective-permute-start | bytes 49160 | tf_op jit(solution)/shard_map/ppermute | solution.py:32
  78.7 9.3 %all-to-all-start.1 = ((f32[4,32,256]{2,1,0:T(8,128)}), f32[4,32,256]{2,1,0:T(8,128)}, u32[]{:S(2)}, u32[]{:S(2)}) async-start(f32[4,32,256]{2,1,0:T(8,128)} %broadcast_in_dim.42), calls=%async_computation.1 | async-start | bytes 262144 | tf_op jit(solution)/shard_map/all_to_all | solution.py:37
  82.7 178.6 %collective-permute-start.4 = (bf16[32,256]{1,0:T(8,128)(2,1)S(1)}, bf16[32,256]{1,0:T(8,128)(2,1)}, u32[]{:S(2)}, u32[]{:S(2)}) collective-permute-start(bf16[32,256]{1,0:T(8,128)(2,1)S(1)} %convolution_convert_fusion.2), channel_id=1, source_target_pairs={{0,4},{1,5},{2,6},{3,7},{4,8},{5,9},{6,10},{7,11},{8,12},{9,13},{1... | collective-permute-start | bytes 49160 | tf_op jit(solution)/shard_map/ppermute | solution.py:32
  89.6 25.7 %all-to-all-start.2 = ((f32[4,32,256]{2,1,0:T(8,128)}), f32[4,32,256]{2,1,0:T(8,128)}, u32[]{:S(2)}, u32[]{:S(2)}) async-start(f32[4,32,256]{2,1,0:T(8,128)} %broadcast_in_dim.43), calls=%async_computation.2 | async-start | bytes 262144 | tf_op jit(solution)/shard_map/all_to_all | solution.py:37
  116.9 133.9 %all-to-all-start.3 = ((bf16[8,32,256]{2,1,0:T(8,128)(2,1)}), bf16[8,32,256]{2,1,0:T(8,128)(2,1)}, u32[]{:S(2)}, u32[]{:S(2)}) async-start(bf16[8,32,256]{2,1,0:T(8,128)(2,1)} %broadcast_in_dim.44), calls=%async_computation.3 | async-start | bytes 262144 | tf_op jit(solution)/shard_map/all_to_all | solution.py:37
  250.8 8.6 %copy-start.7 = (bf16[1,256,256]{2,1,0:T(8,128)(2,1)S(1)}, bf16[1,256,256]{2,1,0:T(8,128)(2,1)}, u32[]{:S(2)}) copy-start(bf16[1,256,256]{2,1,0:T(8,128)(2,1)} %param.17) | copy-start | bytes 393220
  251.9 10.7 %copy-start.2 = (f32[1,32,1024]{2,1,0:T(8,128)S(1)}, f32[1,32,1024]{2,1,0:T(8,128)}, u32[]{:S(2)}) copy-start(f32[1,32,1024]{2,1,0:T(8,128)} %shard_map.118) | copy-start | bytes 393220
  251.9 10.7 %copy-start.3 = (f32[1,32,1024]{2,1,0:T(8,128)S(1)}, f32[1,32,1024]{2,1,0:T(8,128)}, u32[]{:S(2)}) copy-start(f32[1,32,1024]{2,1,0:T(8,128)} %shard_map.119) | copy-start | bytes 393220
  251.9 10.7 %copy-start.4 = (f32[1,32,1024]{2,1,0:T(8,128)S(1)}, f32[1,32,1024]{2,1,0:T(8,128)}, u32[]{:S(2)}) copy-start(f32[1,32,1024]{2,1,0:T(8,128)} %shard_map.120) | copy-start | bytes 393220
  251.9 10.7 %copy-start.5 = (f32[1,32,1024]{2,1,0:T(8,128)S(1)}, f32[1,32,1024]{2,1,0:T(8,128)}, u32[]{:S(2)}) copy-start(f32[1,32,1024]{2,1,0:T(8,128)} %shard_map.121) | copy-start | bytes 393220
  261.3 2.9 %copy-start.16 = (s32[1,1024]{1,0:T(1,128)S(1)}, s32[1,1024]{1,0:T(1,128)}, u32[]{:S(2)}) copy-start(s32[1,1024]{1,0:T(1,128)} %copy-done.15) | copy-start | bytes 12292
  261.3 4.6 %copy-start.14 = (s32[1,1024]{1,0:T(1,128)S(1)}, s32[1,1024]{1,0:T(1,128)}, u32[]{:S(2)}) copy-start(s32[1,1024]{1,0:T(1,128)} %copy-done.13) | copy-start | bytes 12292
  261.3 6.3 %copy-start.12 = (s32[1,1024]{1,0:T(1,128)S(1)}, s32[1,1024]{1,0:T(1,128)}, u32[]{:S(2)}) copy-start(s32[1,1024]{1,0:T(1,128)} %copy-done.11) | copy-start | bytes 12292
  261.3 8.0 %copy-start.10 = (s32[1,1024]{1,0:T(1,128)S(1)}, s32[1,1024]{1,0:T(1,128)}, u32[]{:S(2)}) copy-start(s32[1,1024]{1,0:T(1,128)} %copy-done.9) | copy-start | bytes 12292
